TPU v7x, 512 devices: a whole 4x8x8 slice. The times are simulated.
512 devices in a mesh: row: 16 (over z, core), col: 32 (over y, x).
Axes of the slice: x: 4, y: 8, z: 8, core: 2. Of those that a mesh axis runs over, the one named last changes fastest.
Arguments:
- a11: float32 [256, 256], replicated, may hold values from -1 to 400, as said below
- l11_bar: float32 [256, 256], replicated, may hold values from -24 to 24
- a21: float32 [32768, 256], P(('col', 'row')), may hold values from -72 to 72
- l21_bar: float32 [32768, 256], P(('col', 'row')), may hold values from -6 to 6
- s_bar: bfloat16 [32, 16, 64, 32768], P(None, 'row', None, 'col'), may hold values from -0.0625 to 0.0625
Outputs:
- a21_bar: float32 [32768, 256], P(('col', 'row'))
- a11_bar: float32 [256, 256], replicated
Inputs may be any that keep to these rules, and one draw needn't show every extreme that they name: a11 is symmetric and each diagonal entry exceeds the sum of the magnitudes of the other entries of its row.
All inputs are finite; a program needn't handle non-finite values.
Results may differ from a plain program's by a relative error of at most 0.0036.
Values may be sent and summed in bfloat16 or wider, within the bound.
No kernel may reach another device: no remote copies, remote signals or barrier semaphores. Data moves between devices by JAX's collectives and lax.ppermute only.
A program may use at most 64 MiB of HBM per device.

v0:
```python
import jax
import jax.numpy as jnp
from jax import lax
from jax.sharding import PartitionSpec as P


def halve_lower(square):
    lower = jnp.tril(square)
    return lower - 0.5 * jnp.diag(jnp.diag(square))


def right_solve_t(factor, rhs):
    return lax.linalg.triangular_solve(factor, rhs, left_side=False, lower=True, transpose_a=True)


def right_solve(factor, rhs):
    return lax.linalg.triangular_solve(factor, rhs, left_side=False, lower=True, transpose_a=False)


def left_solve_t(factor, rhs):
    return lax.linalg.triangular_solve(factor, rhs, left_side=True, lower=True, transpose_a=True)


def inner_rows(left, right):
    return lax.dot_general(
        left, right, (((0,), (0,)), ((), ())), preferred_element_type=jnp.float32
    )


def body(a11, l11_bar, a21, l21_bar, s_bar):
    highest = lax.Precision.HIGHEST
    rows_own = a21.shape[0]
    blocks_here = s_bar.shape[0]
    tile = s_bar.reshape(blocks_here * rows_own, s_bar.shape[3])
    l11 = jnp.linalg.cholesky(a11)
    l21_own = right_solve_t(l11, a21)
    panel_own = l21_own.astype(jnp.bfloat16)
    panel_rows = lax.all_gather(panel_own, "col", axis=0, tiled=True)
    panel_cols = lax.all_gather(panel_own, "row", axis=0, tiled=True)
    strip = tile
    row_share = lax.psum_scatter(
        jnp.dot(strip, panel_cols, preferred_element_type=jnp.float32),
        "col",
        scatter_dimension=0,
        tiled=True,
    )
    strip = tile
    col_share = lax.psum_scatter(
        inner_rows(strip, panel_rows), "row", scatter_dimension=0, tiled=True
    )
    trail = l21_bar - row_share - col_share
    a21_bar = right_solve(l11, trail)
    panel_exact = panel_own.astype(jnp.float32)
    coupling = lax.psum(jnp.dot(trail.T, panel_exact, precision=highest), ("row", "col"))
    l11_total = l11_bar - left_solve_t(l11, coupling)
    middle = halve_lower(jnp.dot(l11.T, l11_total, precision=highest))
    left = left_solve_t(l11, middle)
    whole = right_solve(l11, left)
    a11_bar = 0.5 * (whole + whole.T)
    return (a21_bar, a11_bar)


def solution(mesh):
    in_specs = (
        P(),
        P(),
        P(("col", "row"), None),
        P(("col", "row"), None),
        P(None, "row", None, "col"),
    )
    out_specs = (P(("col", "row"), None), P())
    return jax.shard_map(body, mesh=mesh, in_specs=in_specs, out_specs=out_specs, check_vma=False)
```

profile of v0, /device:TPU:1, one launch (start us, length us, event | category | flops | bytes accessed | tf_op | source)
XLA Modules:
  0.0 740.1 jit_solution(10154742874111276805)
XLA Ops:
  7.2 1.1 copy.13
  8.3 1.0 fusion.4
  9.3 11.7 %cholesky.50 = f32[128,128]{1,0:T(8,128)S(1)} custom-call(f32[128,128]{1,0:T(8,128)S(1)} %cholesky.118), custom_call_target="Cholesky" | custom-call | tf_op jit(solution)/shard_map/jit(cholesky)/cholesky | solution.py:35
  21.1 9.8 %custom-call.21 = f32[1,128,128]{1,2,0:T(8,128)S(1)} custom-call(f32[1,128,128]{2,1,0:T(8,128)S(1)} %get-tuple-element.40), custom_call_target="InvertDiagBlocksLowerTriangular" | custom-call | tf_op jit(solution)/shard_map/jit(cholesky)/cholesky | solution.py:35
  31.4 11.7 %cholesky.105 = f32[128,128]{1,0:T(8,128)S(1)} custom-call(f32[128,128]{1,0:T(8,128)S(1)} %convolution_subtract_fusion.3), custom_call_target="Cholesky" | custom-call | tf_op jit(solution)/shard_map/jit(cholesky)/cholesky | solution.py:35
  45.1 4.0 while.5
  45.8 1.3 bitcast_dynamic-update-slice_fusion.2
  47.8 1.3 bitcast_dynamic-update-slice_fusion.2
  49.1 19.7 %custom-call.22 = f32[2,128,128]{1,2,0:T(8,128)S(1)} custom-call(f32[2,128,128]{2,1,0:T(8,128)S(1)} %get-tuple-element.18), custom_call_target="InvertDiagBlocksLowerTriangular" | custom-call | tf_op jit(solution)/shard_map/triangular_solve | solution.py:13
  68.7 0.9 fusion.23
  69.7 1.0 convolution_subtract_fusion.5
  71.6 82.3 %all-gather.2.cloned.1.call-done = bf16[2048,256]{1,0:T(8,128)(2,1)} async-done(((bf16[64,256]{1,0:T(8,128)(2,1)}), bf16[2048,256]{1,0:T(8,128)(2,1)}) %all-gather.2.cloned.1.call-update) | async-done | bytes 1048592 | tf_op jit(solution)/shard_map/all_gather | solution.py:38
  153.9 3.8 convolution_bitcast_fusion.1
  157.7 1.3 copy.19
  159.1 25.0 %all_gather.6 = bf16[1024,256]{1,0:T(8,128)(2,1)S(1)} all-gather(bf16[64,256]{1,0:T(8,128)(2,1)S(1)} %copy-done), channel_id=1, replica_groups=mesh['row'=16,'col'=32] {'row'}, dimensions={0}, use_global_device_ids=true | all-gather | bytes 557056 | tf_op jit(solution)/shard_map/all_gather | solution.py:39
  184.1 3.5 convolution_bitcast_fusion
  187.7 1.9 copy.17
  189.6 31.2 %reduce-scatter.9.cloned.1.call-done = f32[64,256]{1,0:T(8,128)} async-done(((f32[1024,256]{1,0:T(8,128)}), f32[64,256]{1,0:T(8,128)}) %reduce-scatter.9.cloned.1.call-update) | async-done | bytes 65552 | tf_op jit(solution)/shard_map/reduce_scatter | solution.py:48
  220.8 223.8 %reduce-scatter.7.cloned.1.call-done = f32[64,256]{1,0:T(8,128)} async-done(((f32[2048,256]{1,0:T(8,128)}), f32[64,256]{1,0:T(8,128)}) %reduce-scatter.7.cloned.1.call-update) | async-done | bytes 65552 | tf_op jit(solution)/shard_map/reduce_scatter | solution.py:41
  445.6 1.0 fusion.36
  447.9 277.3 %all-reduce.3.cloned.1.call-done = f32[256,256]{1,0:T(8,128)} async-done(((f32[256,256]{1,0:T(8,128)}), f32[256,256]{1,0:T(8,128)}) %all-reduce.3.cloned.1.call-update) | async-done | bytes 262160 | tf_op jit(solution)/shard_map/psum | solution.py:54
  725.2 1.2 fusion.11
  726.4 1.2 convolution_subtract_fusion.2
  728.4 2.3 gather_fusion
  (50 shorter events, 9.3 us)
Async XLA Ops:
  7.2 146.7 %all-gather.2.cloned.1.call-start = ((), (), s32[]{:S(2)}) async-start(), calls=%async_computation.2 | async-start | bytes 1081344 | tf_op jit(solution)/shard_map/all_gather | solution.py:38
  71.6 149.3 %reduce-scatter.9.cloned.1.call-start = ((), (), s32[]{:S(2)}) async-start(), calls=%async_computation.5 | async-start | bytes 1114112 | tf_op jit(solution)/shard_map/reduce_scatter | solution.py:48
  153.9 5.2 copy-start
  159.1 285.6 %reduce-scatter.7.cloned.1.call-start = ((), (), s32[]{:S(2)}) async-start(), calls=%async_computation.4 | async-start | bytes 2162688 | tf_op jit(solution)/shard_map/reduce_scatter | solution.py:41
  187.6 257.0 %copy-start.2 = (f32[64,256]{1,0:T(8,128)S(1)}, f32[64,256]{1,0:T(8,128)}, u32[]{:S(2)}) copy-start(f32[64,256]{1,0:T(8,128)} %param.10) | copy-start | bytes 196612
  187.7 540.2 %copy-start.1 = (f32[256,256]{1,0:T(8,128)S(1)}, f32[256,256]{1,0:T(8,128)}, u32[]{:S(2)}) copy-start(f32[256,256]{1,0:T(8,128)} %param.8) | copy-start | bytes 786436
  189.6 535.7 %all-reduce.3.cloned.1.call-start = ((), (), s32[]{:S(2)}) async-start(), calls=%async_computation.3 | async-start | bytes 524288 | tf_op jit(solution)/shard_map/psum | solution.py:54
Sparse Core Ops, SparseCore 0:
  71.7 82.1 all-gather.1
  159.2 61.6 reduce-scatter.8
  225.3 219.3 reduce-scatter.6
  450.1 275.0 all-reduce.2
where the time goes:
time: 741 us; the launch traced here: 740 us
  waiting for transfers between devices  615 us (83%)
  other arithmetic  57.7 us (8%)
  blocking collectives  25 us (3%)
  matrix products  16.5 us (2%)
  between operations  15.3 us (2%)
  local copies, waits for them, and re-layouts  10.7 us (1%)
    psum x1, waiting for transfers between devices, body(): lax.psum(jnp.dot(trail.T, panel_exact, precision=highest), ('row', 'col'))  277 us
    reduce_scatter x1, waiting for transfers between devices, body(): lax.psum_scatter(jnp.dot(strip, panel_cols, preferred_element_type=jnp.fl...  224 us
    all_gather x1, waiting for transfers between devices, body(): panel_rows = lax.all_gather(panel_own, 'col', axis=0, tiled=True)  82.3 us
    another operation x6, other arithmetic, body(): l11 = jnp.linalg.cholesky(a11)  33.9 us
    reduce_scatter x1, waiting for transfers between devices, body(): lax.psum_scatter(inner_rows(strip, panel_rows), 'row', scatter_dimension=...  31.2 us
    all_gather x1, blocking collectives, body(): panel_cols = lax.all_gather(panel_own, 'row', axis=0, tiled=True)  25 us
    another operation x5, other arithmetic, right_solve_t(): lax.linalg.triangular_solve(factor, rhs, left_side=False, lower=True, tra...  20.3 us
  transfers between devices with their start and end apart: 4, of which 4 were waited for; matrix products, arithmetic and copies ran while one was open for 1% of the time, Pallas kernels for 0%

commit v1 on v0

--- a/solution.py
+++ b/solution.py
@@ -27,31 +27,45 @@
     )
 
 
+def gather_rows(part, axis, size):
+    spread = jnp.broadcast_to(part[None], (size,) + part.shape)
+    return lax.all_to_all(spread, axis, 0, 0, tiled=True).reshape(-1, part.shape[-1])
+
+
+def scatter_sum(whole, axis, size):
+    pieces = whole.reshape(size, -1, whole.shape[-1])
+    return lax.all_to_all(pieces, axis, 0, 0, tiled=True).sum(0)
+
+
+def all_sum(square, axes, size):
+    flat = square.reshape(size, -1)
+    mine = lax.all_to_all(flat, axes, 0, 0, tiled=True).sum(0, keepdims=True)
+    whole = lax.all_to_all(jnp.broadcast_to(mine, flat.shape), axes, 0, 0, tiled=True)
+    return whole.reshape(square.shape)
+
+
 def body(a11, l11_bar, a21, l21_bar, s_bar):
     highest = lax.Precision.HIGHEST
+    n_row = lax.axis_size("row")
+    n_col = lax.axis_size("col")
     rows_own = a21.shape[0]
     blocks_here = s_bar.shape[0]
     tile = s_bar.reshape(blocks_here * rows_own, s_bar.shape[3])
     l11 = jnp.linalg.cholesky(a11)
     l21_own = right_solve_t(l11, a21)
     panel_own = l21_own.astype(jnp.bfloat16)
-    panel_rows = lax.all_gather(panel_own, "col", axis=0, tiled=True)
+    panel_rows = gather_rows(panel_own, "col", n_col)
     panel_cols = lax.all_gather(panel_own, "row", axis=0, tiled=True)
-    strip = tile
-    row_share = lax.psum_scatter(
-        jnp.dot(strip, panel_cols, preferred_element_type=jnp.float32),
-        "col",
-        scatter_dimension=0,
-        tiled=True,
+    row_share = scatter_sum(
+        jnp.dot(tile, panel_cols, preferred_element_type=jnp.float32), "col", n_col
     )
-    strip = tile
-    col_share = lax.psum_scatter(
-        inner_rows(strip, panel_rows), "row", scatter_dimension=0, tiled=True
-    )
+    col_share = scatter_sum(inner_rows(tile, panel_rows), "row", n_row)
     trail = l21_bar - row_share - col_share
     a21_bar = right_solve(l11, trail)
     panel_exact = panel_own.astype(jnp.float32)
-    coupling = lax.psum(jnp.dot(trail.T, panel_exact, precision=highest), ("row", "col"))
+    coupling = all_sum(
+        jnp.dot(trail.T, panel_exact, precision=highest), ("row", "col"), n_row * n_col
+    )
     l11_total = l11_bar - left_solve_t(l11, coupling)
     middle = halve_lower(jnp.dot(l11.T, l11_total, precision=highest))
     left = left_solve_t(l11, middle)

time: 741 us -> 289 us (0.39)
  waiting for transfers between devices: 615 us -> 81 us
  blocking collectives: 25 us -> 75.1 us
  starting transfers between devices: 0.16 us -> 41.8 us
  between operations: 15.3 us -> 2.37 us
    psum x1 -> x0, waiting for transfers between devices: 277 us -> none  [body(): lax.psum(jnp.dot(trail.T, panel_exact, precision=highest), ('row', 'col'))]
    reduce_scatter x2 -> x0, waiting for transfers between devices: 255 us -> none  [the longest x1 224 us: body(): lax.psum_scatter(jnp.dot(strip, panel_cols, preferred_element_type=jnp.fl...]
    all_gather x1 -> x0, waiting for transfers between devices: 82.3 us -> none  [body(): panel_rows = lax.all_gather(panel_own, 'col', axis=0, tiled=True)]
    all_to_all x0 -> x4, waiting for transfers between devices: none -> 81 us  [the longest x2 47.7 us: scatter_sum(): return lax.all_to_all(pieces, axis, 0, 0, tiled=True).sum(0)]
    all_to_all x0 -> x4, starting transfers between devices: none -> 41.8 us  [the longest x2 18.4 us: scatter_sum(): return lax.all_to_all(pieces, axis, 0, 0, tiled=True).sum(0)]
    all_to_all x0 -> x1, blocking collectives: none -> 36.5 us  [gather_rows(): lax.all_to_all(spread, axis, 0, 0, tiled=True).reshape(-1, part.shape[-1])]
    all_gather x1, blocking collectives: 25 us -> 38.6 us  [body(): panel_cols = lax.all_gather(panel_own, 'row', axis=0, tiled=True)]
  transfers between devices with their start and end apart: 4 -> 4, of which waited for: 4 -> 3; matrix products, arithmetic and copies ran while one was open for 1% -> 3% of each run, Pallas kernels for 0% -> 0%
where the time goes in v1:
time: 289 us; the launch traced here: 288 us
  waiting for transfers between devices  81 us (28%)
  blocking collectives  75.1 us (26%)
  other arithmetic  59.8 us (21%)
  starting transfers between devices  41.8 us (14%)
  matrix products  14.4 us (5%)
  local copies, waits for them, and re-layouts  13.8 us (5%)
    all_to_all x2, waiting for transfers between devices, scatter_sum(): return lax.all_to_all(pieces, axis, 0, 0, tiled=True).sum(0)  47.7 us
    all_gather x1, blocking collectives, body(): panel_cols = lax.all_gather(panel_own, 'row', axis=0, tiled=True)  38.6 us
    all_to_all x1, blocking collectives, gather_rows(): lax.all_to_all(spread, axis, 0, 0, tiled=True).reshape(-1, part.shape[-1])  36.5 us
    another operation x6, other arithmetic, body(): l11 = jnp.linalg.cholesky(a11)  34 us
    another operation x5, other arithmetic, right_solve_t(): lax.linalg.triangular_solve(factor, rhs, left_side=False, lower=True, tra...  19.7 us
    all_to_all x2, starting transfers between devices, scatter_sum(): return lax.all_to_all(pieces, axis, 0, 0, tiled=True).sum(0)  18.4 us
    all_to_all x1, waiting for transfers between devices, all_sum(): mine = lax.all_to_all(flat, axes, 0, 0, tiled=True).sum(0, keepdims=True)  17 us
    all_to_all x1, waiting for transfers between devices, all_sum(): lax.all_to_all(jnp.broadcast_to(mine, flat.shape), axes, 0, 0, tiled=True)  16.3 us
  transfers between devices with their start and end apart: 4, of which 3 were waited for; matrix products, arithmetic and copies ran while one was open for 3% of the time, Pallas kernels for 0%

profile of v1, /device:TPU:1, one launch (start us, length us, event | category | flops | bytes accessed | tf_op | source)
XLA Modules:
  0.0 288.4 jit_solution(2026768874578308694)
XLA Ops:
  0.6 1.1 copy.18
  2.7 11.7 %cholesky.50 = f32[128,128]{1,0:T(8,128)S(1)} custom-call(f32[128,128]{1,0:T(8,128)S(1)} %cholesky.118), custom_call_target="Cholesky" | custom-call | tf_op jit(solution)/shard_map/jit(cholesky)/cholesky | solution.py:54
  14.5 9.8 %custom-call.21 = f32[1,128,128]{1,2,0:T(8,128)S(1)} custom-call(f32[1,128,128]{2,1,0:T(8,128)S(1)} %get-tuple-element.40), custom_call_target="InvertDiagBlocksLowerTriangular" | custom-call | tf_op jit(solution)/shard_map/jit(cholesky)/cholesky | solution.py:54
  24.8 11.7 %cholesky.105 = f32[128,128]{1,0:T(8,128)S(1)} custom-call(f32[128,128]{1,0:T(8,128)S(1)} %convolution_subtract_fusion.3), custom_call_target="Cholesky" | custom-call | tf_op jit(solution)/shard_map/jit(cholesky)/cholesky | solution.py:54
  38.7 4.2 %while.5 = (s32[]{:T(128)}, f32[256,256]{1,0:T(8,128)S(1)}, s32[2,2]{1,0:T(2,128)S(1)}, f32[2,128,128]{2,1,0:T(8,128)S(1)}, s32[]{:T(128)}) while((s32[]{:T(128)}, f32[256,256]{1,0:T(8,128)S(1)}, s32[2,2]{1,0:T(2,128)S(1)}, f32[2,128,128]{2,1,0:T(8,128)S(1)}, s32[]{:T(128)}) %tuple.35), condition=%wide.while_cond.1, body=%wide.while_body.1.sunk | while | flops 2 | bytes 131181 | solution.py:13
  39.5 1.4 bitcast_dynamic-update-slice_fusion.2
  41.5 1.4 bitcast_dynamic-update-slice_fusion.2
  43.0 19.7 %custom-call.22 = f32[2,128,128]{1,2,0:T(8,128)S(1)} custom-call(f32[2,128,128]{2,1,0:T(8,128)S(1)} %get-tuple-element.18), custom_call_target="InvertDiagBlocksLowerTriangular" | custom-call | tf_op jit(solution)/shard_map/triangular_solve | solution.py:13
  65.6 36.5 %all_to_all.30 = bf16[32,64,256]{2,1,0:T(8,128)(2,1)S(1)} all-to-all(bf16[32,64,256]{2,1,0:T(8,128)(2,1)S(1)} %broadcast_in_dim.38), channel_id=1, replica_groups=mesh['row'=16,'col'=32] {'col'}, dimensions={0} | all-to-all | bytes 2097152 | tf_op jit(solution)/shard_map/all_to_all | solution.py:32
  102.1 3.5 %convolution_bitcast_fusion.1 = f32[1024,256]{0,1:T(8,128)S(1)} fusion(bf16[2048,256]{1,0:T(8,128)(2,1)S(1)} %bitcast.79, bf16[2048,1024]{1,0:T(8,128)(2,1)} %bitcast.80), kind=kOutput, calls=%fused_computation.4 | convolution fusion | flops 1073741824 | bytes 6291456 | tf_op jit(solution)/shard_map/dot_general | solution.py:25
  105.6 1.3 copy.20
  106.9 13.1 %all-to-all-start.2 = ((f32[16,64,256]{2,1,0:T(8,128)}), f32[16,64,256]{2,1,0:T(8,128)S(1)}, u32[]{:S(2)}, u32[]{:S(2)}) async-start(f32[16,64,256]{2,1,0:T(8,128)} %bitcast.11), calls=%async_computation.2 | async-start | bytes 2097152 | tf_op jit(solution)/shard_map/all_to_all | solution.py:37
  120.0 38.6 %all_gather.3 = bf16[1024,256]{1,0:T(8,128)(2,1)S(1)} all-gather(bf16[64,256]{1,0:T(8,128)(2,1)S(1)} %copy-done.3), channel_id=1, replica_groups=mesh['row'=16,'col'=32] {'row'}, dimensions={0}, use_global_device_ids=true | all-gather | bytes 557056 | tf_op jit(solution)/shard_map/all_gather | solution.py:58
  158.6 3.5 %convolution_bitcast_fusion = f32[2048,256]{0,1:T(8,128)S(1)} fusion(bf16[1024,256]{1,0:T(8,128)(2,1)S(1)} %all_gather.3, bf16[2048,1024]{1,0:T(8,128)(2,1)} %bitcast.81), kind=kOutput, calls=%fused_computation.3 | convolution fusion | flops 1073741824 | bytes 6815744 | tf_op jit(solution)/shard_map/dot_general | solution.py:60
  162.1 1.9 copy.19
  164.0 5.3 %all-to-all-start = ((f32[32,64,256]{2,1,0:T(8,128)}), f32[32,64,256]{2,1,0:T(8,128)S(1)}, u32[]{:S(2)}, u32[]{:S(2)}) async-start(f32[32,64,256]{2,1,0:T(8,128)} %bitcast.8), calls=%async_computation | async-start | bytes 4194304 | tf_op jit(solution)/shard_map/all_to_all | solution.py:37
  170.0 47.7 %all-to-all-done = f32[32,64,256]{2,1,0:T(8,128)S(1)} async-done(((f32[32,64,256]{2,1,0:T(8,128)}), f32[32,64,256]{2,1,0:T(8,128)S(1)}, u32[]{:S(2)}, u32[]{:S(2)}) %all-to-all-start) | async-done | bytes 2097184 | tf_op jit(solution)/shard_map/all_to_all | solution.py:37
  218.8 1.0 fusion.36
  220.5 14.3 %all-to-all-start.3 = ((f32[512,1,128]{2,1,0:T(1,128)}), f32[512,1,128]{2,1,0:T(1,128)S(1)}, u32[]{:S(2)}, u32[]{:S(2)}) async-start(f32[512,1,128]{2,1,0:T(1,128)} %bitcast.14), calls=%async_computation.3 | async-start | bytes 524288 | tf_op jit(solution)/shard_map/all_to_all | solution.py:42
  235.1 17.0 %all-to-all-done.3 = f32[512,1,128]{2,1,0:T(1,128)S(1)} async-done(((f32[512,1,128]{2,1,0:T(1,128)}), f32[512,1,128]{2,1,0:T(1,128)S(1)}, u32[]{:S(2)}, u32[]{:S(2)}) %all-to-all-start.3) | async-done | bytes 262176 | tf_op jit(solution)/shard_map/all_to_all | solution.py:42
  253.5 9.1 %all-to-all-start.4 = ((f32[512,1,128]{2,1,0:T(1,128)}), f32[512,1,128]{2,1,0:T(1,128)S(1)}, u32[]{:S(2)}, u32[]{:S(2)}) async-start(f32[512,1,128]{2,1,0:T(1,128)} %broadcast_in_dim.39), calls=%async_computation.4 | async-start | bytes 524288 | tf_op jit(solution)/shard_map/all_to_all | solution.py:43
  263.7 16.3 %all-to-all-done.4 = f32[512,1,128]{2,1,0:T(1,128)S(1)} async-done(((f32[512,1,128]{2,1,0:T(1,128)}), f32[512,1,128]{2,1,0:T(1,128)S(1)}, u32[]{:S(2)}, u32[]{:S(2)}) %all-to-all-start.4) | async-done | bytes 262176 | tf_op jit(solution)/shard_map/all_to_all | solution.py:43
  280.5 1.3 reduce.16
  283.3 2.3 gather_fusion
  (62 shorter events, 16.3 us)
Async XLA Ops:
  36.6 69.0 %copy-start = (f32[256,256]{1,0:T(8,128)}, f32[256,256]{1,0:T(8,128)S(1)}, u32[]{:S(2)}) copy-start(f32[256,256]{1,0:T(8,128)S(1)} %get-tuple-element.38) | copy-start | bytes 786436
  64.8 42.1 %copy-start.5 = (bf16[64,128]{1,0:T(8,128)(2,1)}, bf16[64,128]{1,0:T(8,128)(2,1)S(1)}, u32[]{:S(2)}) copy-start(bf16[64,128]{1,0:T(8,128)(2,1)S(1)} %convolution_convert_fusion) | copy-start | bytes 49156
  64.8 0.6 copy-start.2
  105.5 14.5 %copy-start.3 = (bf16[64,256]{1,0:T(8,128)(2,1)S(1)}, bf16[64,256]{1,0:T(8,128)(2,1)}, u32[]{:S(2)}) copy-start(bf16[64,256]{1,0:T(8,128)(2,1)} %copy-done.2) | copy-start | bytes 98308
  106.9 57.1 %all-to-all-start.2 = ((f32[16,64,256]{2,1,0:T(8,128)}), f32[16,64,256]{2,1,0:T(8,128)S(1)}, u32[]{:S(2)}, u32[]{:S(2)}) async-start(f32[16,64,256]{2,1,0:T(8,128)} %bitcast.11), calls=%async_computation.2 | async-start | bytes 2097152 | tf_op jit(solution)/shard_map/all_to_all | solution.py:37
  164.0 53.7 %all-to-all-start = ((f32[32,64,256]{2,1,0:T(8,128)}), f32[32,64,256]{2,1,0:T(8,128)S(1)}, u32[]{:S(2)}, u32[]{:S(2)}) async-start(f32[32,64,256]{2,1,0:T(8,128)} %bitcast.8), calls=%async_computation | async-start | bytes 4194304 | tf_op jit(solution)/shard_map/all_to_all | solution.py:37
  170.0 112.7 %copy-start.1 = (f32[256,256]{1,0:T(8,128)S(1)}, f32[256,256]{1,0:T(8,128)}, u32[]{:S(2)}) copy-start(f32[256,256]{1,0:T(8,128)} %copy-done) | copy-start | bytes 786436
  217.8 64.9 %copy-start.4 = (f32[256,256]{1,0:T(8,128)S(1)}, f32[256,256]{1,0:T(8,128)}, u32[]{:S(2)}) copy-start(f32[256,256]{1,0:T(8,128)} %param.8) | copy-start | bytes 786436
  220.5 31.6 %all-to-all-start.3 = ((f32[512,1,128]{2,1,0:T(1,128)}), f32[512,1,128]{2,1,0:T(1,128)S(1)}, u32[]{:S(2)}, u32[]{:S(2)}) async-start(f32[512,1,128]{2,1,0:T(1,128)} %bitcast.14), calls=%async_computation.3 | async-start | bytes 524288 | tf_op jit(solution)/shard_map/all_to_all | solution.py:42
  253.5 26.5 %all-to-all-start.4 = ((f32[512,1,128]{2,1,0:T(1,128)}), f32[512,1,128]{2,1,0:T(1,128)S(1)}, u32[]{:S(2)}, u32[]{:S(2)}) async-start(f32[512,1,128]{2,1,0:T(1,128)} %broadcast_in_dim.39), calls=%async_computation.4 | async-start | bytes 524288 | tf_op jit(solution)/shard_map/all_to_all | solution.py:43

commit v2 on v1

v2 whole, which is shorter than its diff:
```python
import jax
import jax.numpy as jnp
from jax import lax
from jax.sharding import PartitionSpec as P


def halve_lower(square):
    lower = jnp.tril(square)
    return lower - 0.5 * jnp.diag(jnp.diag(square))


def right_solve_t(factor, rhs):
    return lax.linalg.triangular_solve(factor, rhs, left_side=False, lower=True, transpose_a=True)


def right_solve(factor, rhs):
    return lax.linalg.triangular_solve(factor, rhs, left_side=False, lower=True, transpose_a=False)


def left_solve_t(factor, rhs):
    return lax.linalg.triangular_solve(factor, rhs, left_side=True, lower=True, transpose_a=True)


def inner_rows(left, right, precision=None):
    return lax.dot_general(
        left, right, (((0,), (0,)), ((), ())), preferred_element_type=jnp.float32,
        precision=precision,
    )


def gather_rows(part, axis, size):
    spread = jnp.broadcast_to(part[None], (size,) + part.shape)
    return lax.all_to_all(spread, axis, 0, 0, tiled=True).reshape(-1, part.shape[-1])


def split_pair(values):
    high = values.astype(jnp.bfloat16)
    low = (values - high.astype(jnp.float32)).astype(jnp.bfloat16)
    return high, low


def body(a11, l11_bar, a21, l21_bar, s_bar):
    highest = lax.Precision.HIGHEST
    n_row = lax.axis_size("row")
    n_col = lax.axis_size("col")
    rows_own, width = a21.shape
    blocks_here = s_bar.shape[0]
    tile = s_bar.reshape(blocks_here * rows_own, s_bar.shape[3])
    l11 = jnp.linalg.cholesky(a11)
    l21_own = right_solve_t(l11, a21)
    panel_own = l21_own.astype(jnp.bfloat16)
    panel_rows = gather_rows(panel_own, "col", n_col)
    panel_cols = lax.all_gather(panel_own, "row", axis=0, tiled=True)
    forward = jnp.dot(tile, panel_cols, preferred_element_type=jnp.float32)
    backward = inner_rows(tile, panel_rows)
    panel_exact = panel_own.astype(jnp.float32)
    coupling_part = (
        inner_rows(l21_bar, panel_exact, highest)
        - inner_rows(forward, panel_rows.astype(jnp.float32), highest)
        - inner_rows(backward, panel_cols.astype(jnp.float32), highest)
    )
    high, low = split_pair(coupling_part)
    strip = width // n_col
    pieces = jnp.concatenate(
        [
            forward.astype(jnp.bfloat16).reshape(n_col, rows_own, width),
            high.reshape(n_col, strip, width),
            low.reshape(n_col, strip, width),
        ],
        axis=1,
    )
    got = lax.all_to_all(pieces, "col", 0, 0, tiled=True).astype(jnp.float32)
    row_share = got[:, :rows_own].sum(0)
    coupling_col = (got[:, rows_own:rows_own + strip] + got[:, rows_own + strip:]).sum(0)
    span = width // n_row
    spread = coupling_col.reshape(strip, n_row, span).transpose(1, 0, 2).reshape(n_row, strip * span)
    high, low = split_pair(spread)
    pieces = jnp.concatenate(
        [
            backward.astype(jnp.bfloat16).reshape(n_row, rows_own, width),
            jnp.concatenate([high, low], axis=1).reshape(n_row, 1, 2 * strip * span),
        ],
        axis=1,
    )
    got = lax.all_to_all(pieces, "row", 0, 0, tiled=True).astype(jnp.float32)
    col_share = got[:, :rows_own].sum(0)
    mine = (got[:, rows_own, : strip * span] + got[:, rows_own, strip * span:]).sum(0)
    n_all = n_row * n_col
    blocks = lax.all_to_all(
        jnp.broadcast_to(mine[None], (n_all, strip * span)), ("row", "col"), 0, 0, tiled=True
    )
    coupling = (
        blocks.reshape(n_row, n_col, strip, span).transpose(1, 2, 0, 3).reshape(width, width)
    )
    trail = l21_bar - row_share - col_share
    a21_bar = right_solve(l11, trail)
    l11_total = l11_bar - left_solve_t(l11, coupling)
    middle = halve_lower(jnp.dot(l11.T, l11_total, precision=highest))
    left = left_solve_t(l11, middle)
    whole = right_solve(l11, left)
    a11_bar = 0.5 * (whole + whole.T)
    return (a21_bar, a11_bar)


def solution(mesh):
    in_specs = (
        P(),
        P(),
        P(("col", "row"), None),
        P(("col", "row"), None),
        P(None, "row", None, "col"),
    )
    out_specs = (P(("col", "row"), None), P())
    return jax.shard_map(body, mesh=mesh, in_specs=in_specs, out_specs=out_specs, check_vma=False)
```

time: 289 us -> 228 us (0.79)
  blocking collectives: 75.1 us -> 25.4 us
  waiting for transfers between devices: 81 us -> 67 us
  starting transfers between devices: 41.8 us -> 35.1 us
  local copies, waits for them, and re-layouts: 13.8 us -> 18.7 us
    all_to_all x1 -> x0, blocking collectives: 36.5 us -> none  [gather_rows(): lax.all_to_all(spread, axis, 0, 0, tiled=True).reshape(-1, part.shape[-1])]
    all_to_all x4, waiting for transfers between devices: 81 us -> 67 us  [the longest x1 32.2 us: body(): got = lax.all_to_all(pieces, 'col', 0, 0, tiled=True).astype(jnp.float32)]
    all_gather x1, blocking collectives: 38.6 us -> 25.4 us  [body(): panel_cols = lax.all_gather(panel_own, 'row', axis=0, tiled=True)]
    all_to_all x4, starting transfers between devices: 41.8 us -> 35.1 us  [the longest x1 10.5 us: gather_rows(): lax.all_to_all(spread, axis, 0, 0, tiled=True).reshape(-1, part.shape[-1])]
    convert_element_type x0 -> x5, other arithmetic: none -> 3.99 us  [the longest x1 1.63 us: body(): got = lax.all_to_all(pieces, 'col', 0, 0, tiled=True).astype(jnp.float32)]
    dot_general x1 -> x4, matrix products: 3.46 us -> 7.11 us  [inner_rows(): lax.dot_general(left, right, (((0,), (0,)), ((), ())), preferred_element_...]
    transpose x0 -> x2, local copies, waits for them, and re-layouts: none -> 3.45 us  [the longest x1 1.96 us: body(): blocks.reshape(n_row, n_col, strip, span).transpose(1, 2, 0, 3)]
    dot_general x2 -> x0, local copies, waits for them, and re-layouts: 3.2 us -> none  [the longest x1 1.88 us: body(): jnp.dot(tile, panel_cols, preferred_element_type=jnp.float32)]
  transfers between devices with their start and end apart: 4 -> 4, of which waited for: 3 -> 3; matrix products, arithmetic and copies ran while one was open for 3% -> 5% of each run, Pallas kernels for 0% -> 0%
where the time goes in v2:
time: 228 us; the launch traced here: 227 us
  waiting for transfers between devices  67 us (29%)
  other arithmetic  62.5 us (27%)
  starting transfers between devices  35.1 us (15%)
  blocking collectives  25.4 us (11%)
  local copies, waits for them, and re-layouts  18.7 us (8%)
  matrix products  15.7 us (7%)
  between operations  2.45 us (1%)
    another operation x6, other arithmetic, body(): l11 = jnp.linalg.cholesky(a11)  34 us
    all_to_all x1, waiting for transfers between devices, body(): got = lax.all_to_all(pieces, 'col', 0, 0, tiled=True).astype(jnp.float32)  32.2 us
    all_gather x1, blocking collectives, body(): panel_cols = lax.all_gather(panel_own, 'row', axis=0, tiled=True)  25.4 us
    another operation x5, other arithmetic, right_solve_t(): lax.linalg.triangular_solve(factor, rhs, left_side=False, lower=True, tra...  19.7 us
    all_to_all x1, waiting for transfers between devices, body(): got = lax.all_to_all(pieces, 'row', 0, 0, tiled=True).astype(jnp.float32)  18.7 us
    all_to_all x1, waiting for transfers between devices, body(): lax.all_to_all(jnp.broadcast_to(mine[None], (n_all, strip * span)), ('row...  16.2 us
    all_to_all x1, starting transfers between devices, gather_rows(): lax.all_to_all(spread, axis, 0, 0, tiled=True).reshape(-1, part.shape[-1])  10.5 us
    all_to_all x1, starting transfers between devices, body(): got = lax.all_to_all(pieces, 'col', 0, 0, tiled=True).astype(jnp.float32)  9.61 us
  transfers between devices with their start and end apart: 4, of which 3 were waited for; matrix products, arithmetic and copies ran while one was open for 5% of the time, Pallas kernels for 0%

profile of v2, /device:TPU:1, one launch (start us, length us, event | category | flops | bytes accessed | tf_op | source)
XLA Modules:
  0.0 227.0 jit_solution(4877699336866302328)
XLA Ops:
  2.8 11.7 %cholesky.50 = f32[128,128]{1,0:T(8,128)S(1)} custom-call(f32[128,128]{1,0:T(8,128)S(1)} %cholesky.118), custom_call_target="Cholesky" | custom-call | tf_op jit(solution)/shard_map/jit(cholesky)/cholesky | solution.py:49
  14.5 9.8 %custom-call.21 = f32[1,128,128]{1,2,0:T(8,128)S(1)} custom-call(f32[1,128,128]{2,1,0:T(8,128)S(1)} %get-tuple-element.44), custom_call_target="InvertDiagBlocksLowerTriangular" | custom-call | tf_op jit(solution)/shard_map/jit(cholesky)/cholesky | solution.py:49
  24.8 11.7 %cholesky.105 = f32[128,128]{1,0:T(8,128)S(1)} custom-call(f32[128,128]{1,0:T(8,128)S(1)} %convolution_subtract_fusion.5), custom_call_target="Cholesky" | custom-call | tf_op jit(solution)/shard_map/jit(cholesky)/cholesky | solution.py:49
  38.6 4.1 %while.5 = (s32[]{:T(128)}, f32[256,256]{1,0:T(8,128)S(1)}, s32[2,2]{1,0:T(2,128)S(1)}, f32[2,128,128]{2,1,0:T(8,128)S(1)}, s32[]{:T(128)}) while((s32[]{:T(128)}, f32[256,256]{1,0:T(8,128)S(1)}, s32[2,2]{1,0:T(2,128)S(1)}, f32[2,128,128]{2,1,0:T(8,128)S(1)}, s32[]{:T(128)}) %tuple.37), condition=%wide.while_cond.1, body=%wide.while_body.1.sunk | while | flops 2 | bytes 131189 | solution.py:13
  39.3 1.4 bitcast_dynamic-update-slice_fusion.2
  41.3 1.4 bitcast_dynamic-update-slice_fusion.2
  42.7 19.7 %custom-call.22 = f32[2,128,128]{1,2,0:T(8,128)S(1)} custom-call(f32[2,128,128]{2,1,0:T(8,128)S(1)} %get-tuple-element.18), custom_call_target="InvertDiagBlocksLowerTriangular" | custom-call | tf_op jit(solution)/shard_map/triangular_solve | solution.py:13
  64.1 10.5 %all-to-all-start = ((bf16[32,64,256]{2,1,0:T(8,128)(2,1)}), bf16[32,64,256]{2,1,0:T(8,128)(2,1)S(1)}, u32[]{:S(2)}, u32[]{:S(2)}) async-start(bf16[32,64,256]{2,1,0:T(8,128)(2,1)} %broadcast_in_dim.38), calls=%async_computation | async-start | bytes 2097152 | tf_op jit(solution)/shard_map/all_to_all | solution.py:33
  74.6 25.4 %all_gather.3 = bf16[1024,256]{1,0:T(8,128)(2,1)S(1)} all-gather(bf16[64,256]{1,0:T(8,128)(2,1)S(1)} %pad_maximum_fusion.6), channel_id=1, replica_groups=mesh['row'=16,'col'=32] {'row'}, dimensions={0}, use_global_device_ids=true | all-gather | bytes 557056 | tf_op jit(solution)/shard_map/all_gather | solution.py:53
  100.0 3.7 %fusion.40 = f32[256,2048]{1,0:T(8,128)S(1)} fusion(bf16[1024,256]{1,0:T(8,128)(2,1)S(1)} %all_gather.3, bf16[2048,1024]{1,0:T(8,128)(2,1)} %bitcast.102), kind=kOutput, calls=%fused_computation.93 | convolution fusion | flops 1073741824 | bytes 6815744 | tf_op jit(solution)/shard_map/dot_general | solution.py:54
  104.9 2.3 copy.25
  107.1 1.9 convolution_bitcast_fusion
  109.0 3.5 %fusion.41 = f32[256,1024]{1,0:T(8,128)S(1)} fusion(bf16[2048,256]{1,0:T(8,128)(2,1)S(1)} %bitcast.97, bf16[2048,1024]{1,0:T(8,128)(2,1)} %bitcast.103), kind=kOutput, calls=%fused_computation.94 | convolution fusion | flops 1073741824 | bytes 6291456 | tf_op jit(solution)/shard_map/dot_general | solution.py:25
  114.6 1.2 pad_maximum_fusion
  115.8 9.6 %all-to-all-start.1 = ((bf16[32,80,256]{2,1,0:T(8,128)(2,1)}), bf16[32,80,256]{2,1,0:T(8,128)(2,1)}, u32[]{:S(2)}, u32[]{:S(2)}) async-start(bf16[32,80,256]{2,1,0:T(8,128)(2,1)} %pad_maximum_fusion), calls=%async_computation.1 | async-start | bytes 2621440 | tf_op jit(solution)/shard_map/all_to_all | solution.py:72
  125.7 32.2 %all-to-all-done.1 = bf16[32,80,256]{2,1,0:T(8,128)(2,1)} async-done(((bf16[32,80,256]{2,1,0:T(8,128)(2,1)}), bf16[32,80,256]{2,1,0:T(8,128)(2,1)}, u32[]{:S(2)}, u32[]{:S(2)}) %all-to-all-start.1) | async-done | bytes 1310752 | tf_op jit(solution)/shard_map/all_to_all | solution.py:72
  157.9 1.6 convert_element_type.49
  160.3 1.5 copy.27
  163.6 6.0 %all-to-all-start.2 = ((bf16[16,65,256]{2,1,0:T(8,128)(2,1)}), bf16[16,65,256]{2,1,0:T(8,128)(2,1)}, u32[]{:S(2)}, u32[]{:S(2)}) async-start(bf16[16,65,256]{2,1,0:T(8,128)(2,1)} %pad_maximum_fusion.1), calls=%async_computation.2 | async-start | bytes 1179648 | tf_op jit(solution)/shard_map/all_to_all | solution.py:85
  169.8 18.7 %all-to-all-done.2 = bf16[16,65,256]{2,1,0:T(8,128)(2,1)} async-done(((bf16[16,65,256]{2,1,0:T(8,128)(2,1)}), bf16[16,65,256]{2,1,0:T(8,128)(2,1)}, u32[]{:S(2)}, u32[]{:S(2)}) %all-to-all-start.2) | async-done | bytes 532512 | tf_op jit(solution)/shard_map/all_to_all | solution.py:85
  190.8 9.0 %all-to-all-start.3 = ((f32[512,1,128]{2,1,0:T(1,128)}), f32[512,1,128]{2,1,0:T(1,128)S(1)}, u32[]{:S(2)}, u32[]{:S(2)}) async-start(f32[512,1,128]{2,1,0:T(1,128)} %broadcast_in_dim.39), calls=%async_computation.3 | async-start | bytes 524288 | tf_op jit(solution)/shard_map/all_to_all | solution.py:89
  200.9 16.2 %all-to-all-done.3 = f32[512,1,128]{2,1,0:T(1,128)S(1)} async-done(((f32[512,1,128]{2,1,0:T(1,128)}), f32[512,1,128]{2,1,0:T(1,128)S(1)}, u32[]{:S(2)}, u32[]{:S(2)}) %all-to-all-start.3) | async-done | bytes 262176 | tf_op jit(solution)/shard_map/all_to_all | solution.py:89
  217.5 2.0 copy.30
  221.8 2.3 %gather_fusion = f32[256]{0:T(256)S(1)} fusion(f32[256,256]{1,0:T(8,128)S(1)} %fusion.1, s32[256]{0:T(256)S(1)} %bitcast.95), kind=kCustom, calls=%fused_computation | custom fusion | bytes 4096 | tf_op jit(solution)/shard_map/jit(_diag)/jit(diagonal)/cond/branch_0_fun/gather | solution.py:9
  (88 shorter events, 21.4 us)
Async XLA Ops:
  0.6 61.7 %copy-start.11 = (f32[64,256]{1,0:T(8,128)S(1)}, f32[64,256]{1,0:T(8,128)}, u32[]{:S(2)}) copy-start(f32[64,256]{1,0:T(8,128)} %param.9) | copy-start | bytes 196612
  36.6 27.6 %copy-start.3 = (f32[256,256]{1,0:T(8,128)}, f32[256,256]{1,0:T(8,128)S(1)}, u32[]{:S(2)}) copy-start(f32[256,256]{1,0:T(8,128)S(1)} %get-tuple-element.42) | copy-start | bytes 786436
  63.0 1.1 copy-start.10
  64.1 44.9 %all-to-all-start = ((bf16[32,64,256]{2,1,0:T(8,128)(2,1)}), bf16[32,64,256]{2,1,0:T(8,128)(2,1)S(1)}, u32[]{:S(2)}, u32[]{:S(2)}) async-start(bf16[32,64,256]{2,1,0:T(8,128)(2,1)} %broadcast_in_dim.38), calls=%async_computation | async-start | bytes 2097152 | tf_op jit(solution)/shard_map/all_to_all | solution.py:33
  100.0 3.7 %copy-start.5 = (bf16[1024,256]{1,0:T(8,128)(2,1)}, bf16[1024,256]{1,0:T(8,128)(2,1)S(1)}, u32[]{:S(2)}) copy-start(bf16[1024,256]{1,0:T(8,128)(2,1)S(1)} %all_gather.3) | copy-start | bytes 1572868
  109.0 3.5 %copy-start.7 = (f32[256,256]{1,0:T(8,128)S(1)}, f32[256,256]{1,0:T(8,128)}, u32[]{:S(2)}) copy-start(f32[256,256]{1,0:T(8,128)} %convolution_bitcast_fusion) | copy-start | bytes 786436
  112.5 2.1 copy-start.1
  112.5 1.4 copy-start.6
  112.6 2.1 copy-start
  114.6 10.8 %copy-start.2 = (f32[256,1024]{1,0:T(8,128)S(1)}, f32[256,1024]{1,0:T(8,128)}, u32[]{:S(2)}) copy-start(f32[256,1024]{1,0:T(8,128)} %copy-done.1) | copy-start | bytes 3145732
  115.8 42.1 %all-to-all-start.1 = ((bf16[32,80,256]{2,1,0:T(8,128)(2,1)}), bf16[32,80,256]{2,1,0:T(8,128)(2,1)}, u32[]{:S(2)}, u32[]{:S(2)}) async-start(bf16[32,80,256]{2,1,0:T(8,128)(2,1)} %pad_maximum_fusion), calls=%async_computation.1 | async-start | bytes 2621440 | tf_op jit(solution)/shard_map/all_to_all | solution.py:72
  163.6 24.8 %all-to-all-start.2 = ((bf16[16,65,256]{2,1,0:T(8,128)(2,1)}), bf16[16,65,256]{2,1,0:T(8,128)(2,1)}, u32[]{:S(2)}, u32[]{:S(2)}) async-start(bf16[16,65,256]{2,1,0:T(8,128)(2,1)} %pad_maximum_fusion.1), calls=%async_computation.2 | async-start | bytes 1179648 | tf_op jit(solution)/shard_map/all_to_all | solution.py:85
  169.7 20.1 %copy-start.9 = (f32[64,256]{1,0:T(8,128)S(1)}, f32[64,256]{1,0:T(8,128)}, u32[]{:S(2)}) copy-start(f32[64,256]{1,0:T(8,128)} %param.10) | copy-start | bytes 196612
  190.8 26.3 %all-to-all-start.3 = ((f32[512,1,128]{2,1,0:T(1,128)}), f32[512,1,128]{2,1,0:T(1,128)S(1)}, u32[]{:S(2)}, u32[]{:S(2)}) async-start(f32[512,1,128]{2,1,0:T(1,128)} %broadcast_in_dim.39), calls=%async_computation.3 | async-start | bytes 524288 | tf_op jit(solution)/shard_map/all_to_all | solution.py:89
  219.5 1.8 copy-start.4
  219.5 1.8 copy-start.8

commit v3 on v2

--- a/solution.py
+++ b/solution.py
@@ -19,6 +19,27 @@
 
 def left_solve_t(factor, rhs):
     return lax.linalg.triangular_solve(factor, rhs, left_side=True, lower=True, transpose_a=True)
+
+
+def invert_lower(factor):
+    eye = jnp.eye(factor.shape[0], dtype=factor.dtype)
+    return lax.linalg.triangular_solve(factor, eye, left_side=True, lower=True)
+
+
+def factor_and_invert(square):
+    highest = lax.Precision.HIGHEST
+    half = square.shape[0] // 2
+    first = lax.linalg.cholesky(square[:half, :half], symmetrize_input=False)
+    first_inv = invert_lower(first)
+    below = jnp.dot(square[half:, :half], first_inv.T, precision=highest)
+    rest = square[half:, half:] - jnp.dot(below, below.T, precision=highest)
+    last = lax.linalg.cholesky(rest, symmetrize_input=False)
+    last_inv = invert_lower(last)
+    corner = -jnp.dot(jnp.dot(last_inv, below, precision=highest), first_inv, precision=highest)
+    zeros = jnp.zeros((half, square.shape[0] - half), square.dtype)
+    factor = jnp.block([[first, zeros], [below, last]])
+    inverse = jnp.block([[first_inv, zeros], [corner, last_inv]])
+    return factor, inverse
 
 
 def inner_rows(left, right, precision=None):
@@ -46,8 +67,8 @@
     rows_own, width = a21.shape
     blocks_here = s_bar.shape[0]
     tile = s_bar.reshape(blocks_here * rows_own, s_bar.shape[3])
-    l11 = jnp.linalg.cholesky(a11)
-    l21_own = right_solve_t(l11, a21)
+    l11, inverse = factor_and_invert(a11)
+    l21_own = jnp.dot(a21, inverse.T, precision=highest)
     panel_own = l21_own.astype(jnp.bfloat16)
     panel_rows = gather_rows(panel_own, "col", n_col)
     panel_cols = lax.all_gather(panel_own, "row", axis=0, tiled=True)
@@ -93,11 +114,11 @@
         blocks.reshape(n_row, n_col, strip, span).transpose(1, 2, 0, 3).reshape(width, width)
     )
     trail = l21_bar - row_share - col_share
-    a21_bar = right_solve(l11, trail)
-    l11_total = l11_bar - left_solve_t(l11, coupling)
+    a21_bar = jnp.dot(trail, inverse, precision=highest)
+    l11_total = l11_bar - jnp.dot(inverse.T, coupling, precision=highest)
     middle = halve_lower(jnp.dot(l11.T, l11_total, precision=highest))
-    left = left_solve_t(l11, middle)
-    whole = right_solve(l11, left)
+    left = jnp.dot(inverse.T, middle, precision=highest)
+    whole = jnp.dot(left, inverse, precision=highest)
     a11_bar = 0.5 * (whole + whole.T)
     return (a21_bar, a11_bar)
 

time: 228 us -> 213 us (0.934)
  other arithmetic: 62.5 us -> 53.1 us
  local copies, waits for them, and re-layouts: 18.7 us -> 15.9 us
    another operation x13 -> x10, other arithmetic: 54.3 us -> 47.1 us  [the longest x4 22.3 us: invert_lower(): return lax.linalg.triangular_solve(factor, eye, left_side=True, lower=True)]
    dot_general x0 -> x9, matrix products: none -> 5.43 us  [the longest x1 1.13 us: factor_and_invert(): rest = square[half:, half:] - jnp.dot(below, below.T, precision=highest)]
    another operation x10 -> x1, local copies, waits for them, and re-layouts: 4.12 us -> 0.09 us  [invert_lower(): return lax.linalg.triangular_solve(factor, eye, left_side=True, lower=True)]
    another operation x17 -> x2, matrix products: 4.37 us -> 0.55 us  [invert_lower(): return lax.linalg.triangular_solve(factor, eye, left_side=True, lower=True)]
where the time goes in v3:
time: 213 us; the launch traced here: 212 us
  waiting for transfers between devices  65.2 us (31%)
  other arithmetic  53.1 us (25%)
  starting transfers between devices  34.5 us (16%)
  blocking collectives  25.4 us (12%)
  matrix products  17.3 us (8%)
  local copies, waits for them, and re-layouts  15.9 us (7%)
    all_to_all x1, waiting for transfers between devices, body(): got = lax.all_to_all(pieces, 'col', 0, 0, tiled=True).astype(jnp.float32)  32.2 us
    all_gather x1, blocking collectives, body(): panel_cols = lax.all_gather(panel_own, 'row', axis=0, tiled=True)  25.4 us
    another operation x4, other arithmetic, invert_lower(): return lax.linalg.triangular_solve(factor, eye, left_side=True, lower=True)  22.3 us
    all_to_all x1, waiting for transfers between devices, body(): got = lax.all_to_all(pieces, 'row', 0, 0, tiled=True).astype(jnp.float32)  18 us
    all_to_all x1, waiting for transfers between devices, body(): lax.all_to_all(jnp.broadcast_to(mine[None], (n_all, strip * span)), ('row...  15 us
    another operation x3, other arithmetic, factor_and_invert(): last = lax.linalg.cholesky(rest, symmetrize_input=False)  12.4 us
    another operation x3, other arithmetic, factor_and_invert(): first = lax.linalg.cholesky(square[:half, :half], symmetrize_input=False)  12.4 us
    all_to_all x1, starting transfers between devices, gather_rows(): lax.all_to_all(spread, axis, 0, 0, tiled=True).reshape(-1, part.shape[-1])  10.5 us
  transfers between devices with their start and end apart: 4, of which 3 were waited for; matrix products, arithmetic and copies ran while one was open for 5% of the time, Pallas kernels for 0%

profile of v3, /device:TPU:1, one launch (start us, length us, event | category | flops | bytes accessed | tf_op | source)
XLA Modules:
  0.0 212.4 jit_solution(5683427228027168117)
XLA Ops:
  1.5 11.7 %custom-call.10 = f32[128,128]{1,0:T(8,128)S(1)} custom-call(f32[128,128]{1,0:T(8,128)S(1)} %slice.31), custom_call_target="Cholesky" | custom-call | tf_op jit(solution)/shard_map/cholesky/custom-call.1 | solution.py:32
  13.9 1.3 select_bitcast_fusion.1
  15.2 9.8 %custom-call.11 = f32[1,128,128]{1,2,0:T(8,128)S(1)} custom-call(f32[1,128,128]{2,1,0:T(8,128)S(1)} %get-tuple-element.8), custom_call_target="InvertDiagBlocksLowerTriangular" | custom-call | tf_op jit(solution)/shard_map/triangular_solve/custom-call.0 | solution.py:26
  26.4 1.1 convolution_subtract_fusion.3
  27.5 11.7 %custom-call.12 = f32[128,128]{1,0:T(8,128)S(1)} custom-call(f32[128,128]{1,0:T(8,128)S(1)} %convolution_subtract_fusion.3), custom_call_target="Cholesky" | custom-call | tf_op jit(solution)/shard_map/cholesky/custom-call.1 | solution.py:36
  39.9 1.3 select_bitcast_fusion
  41.2 10.0 %custom-call.13 = f32[1,128,128]{1,2,0:T(8,128)S(1)} custom-call(f32[1,128,128]{2,1,0:T(8,128)S(1)} %get-tuple-element.6), custom_call_target="InvertDiagBlocksLowerTriangular" | custom-call | tf_op jit(solution)/shard_map/triangular_solve/custom-call.0 | solution.py:26
  53.5 10.5 %all-to-all-start = ((bf16[32,64,256]{2,1,0:T(8,128)(2,1)}), bf16[32,64,256]{2,1,0:T(8,128)(2,1)S(1)}, u32[]{:S(2)}, u32[]{:S(2)}) async-start(bf16[32,64,256]{2,1,0:T(8,128)(2,1)} %broadcast_in_dim.38), calls=%async_computation | async-start | bytes 2097152 | tf_op jit(solution)/shard_map/all_to_all | solution.py:54
  64.0 25.4 %all_gather.3 = bf16[1024,256]{1,0:T(8,128)(2,1)S(1)} all-gather(bf16[64,256]{1,0:T(8,128)(2,1)S(1)} %bitcast.67), channel_id=1, replica_groups=mesh['row'=16,'col'=32] {'row'}, dimensions={0}, use_global_device_ids=true | all-gather | bytes 557056 | tf_op jit(solution)/shard_map/all_gather | solution.py:74
  89.4 3.7 %fusion.39 = f32[256,2048]{1,0:T(8,128)S(1)} fusion(bf16[1024,256]{1,0:T(8,128)(2,1)S(1)} %all_gather.3, bf16[2048,1024]{1,0:T(8,128)(2,1)} %bitcast.70), kind=kOutput, calls=%fused_computation.74 | convolution fusion | flops 1073741824 | bytes 6815744 | tf_op jit(solution)/shard_map/dot_general | solution.py:75
  93.1 1.1 convert_bitcast_fusion
  94.3 2.3 %copy.32 = bf16[2048,256]{1,0:T(8,128)(2,1)} copy(bf16[2048,256]{0,1:T(8,128)(2,1)} %convert_bitcast_fusion) | data formatting | bytes 2097152 | tf_op jit(solution)/shard_map/convert_element_type | solution.py:87
  96.5 1.9 convolution_bitcast_fusion
  98.4 3.5 %fusion.40 = f32[256,1024]{1,0:T(8,128)S(1)} fusion(bf16[2048,256]{1,0:T(8,128)(2,1)S(1)} %bitcast.62, bf16[2048,1024]{1,0:T(8,128)(2,1)} %bitcast.71), kind=kOutput, calls=%fused_computation.75 | convolution fusion | flops 1073741824 | bytes 6291456 | tf_op jit(solution)/shard_map/dot_general | solution.py:46
  104.0 1.2 pad_maximum_fusion
  105.2 9.6 %all-to-all-start.1 = ((bf16[32,80,256]{2,1,0:T(8,128)(2,1)}), bf16[32,80,256]{2,1,0:T(8,128)(2,1)}, u32[]{:S(2)}, u32[]{:S(2)}) async-start(bf16[32,80,256]{2,1,0:T(8,128)(2,1)} %pad_maximum_fusion), calls=%async_computation.1 | async-start | bytes 2621440 | tf_op jit(solution)/shard_map/all_to_all | solution.py:93
  115.1 32.2 %all-to-all-done.1 = bf16[32,80,256]{2,1,0:T(8,128)(2,1)} async-done(((bf16[32,80,256]{2,1,0:T(8,128)(2,1)}), bf16[32,80,256]{2,1,0:T(8,128)(2,1)}, u32[]{:S(2)}, u32[]{:S(2)}) %all-to-all-start.1) | async-done | bytes 1310752 | tf_op jit(solution)/shard_map/all_to_all | solution.py:93
  147.3 1.6 convert_element_type.59
  151.5 5.4 %all-to-all-start.2 = ((bf16[16,65,256]{2,1,0:T(8,128)(2,1)}), bf16[16,65,256]{2,1,0:T(8,128)(2,1)S(1)}, u32[]{:S(2)}, u32[]{:S(2)}) async-start(bf16[16,65,256]{2,1,0:T(8,128)(2,1)} %pad_maximum_fusion.1), calls=%async_computation.2 | async-start | bytes 1179648 | tf_op jit(solution)/shard_map/all_to_all | solution.py:106
  157.7 18.0 %all-to-all-done.2 = bf16[16,65,256]{2,1,0:T(8,128)(2,1)S(1)} async-done(((bf16[16,65,256]{2,1,0:T(8,128)(2,1)}), bf16[16,65,256]{2,1,0:T(8,128)(2,1)S(1)}, u32[]{:S(2)}, u32[]{:S(2)}) %all-to-all-start.2) | async-done | bytes 532512 | tf_op jit(solution)/shard_map/all_to_all | solution.py:106
  177.7 9.0 %all-to-all-start.3 = ((f32[512,1,128]{2,1,0:T(1,128)}), f32[512,1,128]{2,1,0:T(1,128)S(1)}, u32[]{:S(2)}, u32[]{:S(2)}) async-start(f32[512,1,128]{2,1,0:T(1,128)} %broadcast_in_dim.39), calls=%async_computation.3 | async-start | bytes 524288 | tf_op jit(solution)/shard_map/all_to_all | solution.py:110
  188.9 15.0 %all-to-all-done.3 = f32[512,1,128]{2,1,0:T(1,128)S(1)} async-done(((f32[512,1,128]{2,1,0:T(1,128)}), f32[512,1,128]{2,1,0:T(1,128)S(1)}, u32[]{:S(2)}, u32[]{:S(2)}) %all-to-all-start.3) | async-done | bytes 262176 | tf_op jit(solution)/shard_map/all_to_all | solution.py:110
  204.3 1.8 copy.38
  208.2 2.3 %gather_fusion = f32[256]{0:T(256)S(1)} fusion(f32[256,256]{1,0:T(8,128)S(1)} %fusion, s32[256]{0:T(256)S(1)} %bitcast.60), kind=kCustom, calls=%fused_computation | custom fusion | bytes 4096 | tf_op jit(solution)/shard_map/jit(_diag)/jit(diagonal)/cond/branch_0_fun/gather | solution.py:9
  (71 shorter events, 19.9 us)
Async XLA Ops:
  0.6 51.4 %copy-start = (f32[64,256]{1,0:T(8,128)S(1)}, f32[64,256]{1,0:T(8,128)}, u32[]{:S(2)}) copy-start(f32[64,256]{1,0:T(8,128)} %param.10) | copy-start | bytes 196612
  53.5 44.9 %all-to-all-start = ((bf16[32,64,256]{2,1,0:T(8,128)(2,1)}), bf16[32,64,256]{2,1,0:T(8,128)(2,1)S(1)}, u32[]{:S(2)}, u32[]{:S(2)}) async-start(bf16[32,64,256]{2,1,0:T(8,128)(2,1)} %broadcast_in_dim.38), calls=%async_computation | async-start | bytes 2097152 | tf_op jit(solution)/shard_map/all_to_all | solution.py:54
  89.4 3.7 %copy-start.6 = (bf16[1024,256]{1,0:T(8,128)(2,1)}, bf16[1024,256]{1,0:T(8,128)(2,1)S(1)}, u32[]{:S(2)}) copy-start(bf16[1024,256]{1,0:T(8,128)(2,1)S(1)} %all_gather.3) | copy-start | bytes 1572868
  98.4 3.5 %copy-start.8 = (f32[256,256]{1,0:T(8,128)S(1)}, f32[256,256]{1,0:T(8,128)}, u32[]{:S(2)}) copy-start(f32[256,256]{1,0:T(8,128)} %convolution_bitcast_fusion) | copy-start | bytes 786436
  101.9 2.1 copy-start.4
  101.9 1.4 copy-start.7
  101.9 2.1 copy-start.3
  104.0 10.8 %copy-start.5 = (f32[256,1024]{1,0:T(8,128)S(1)}, f32[256,1024]{1,0:T(8,128)}, u32[]{:S(2)}) copy-start(f32[256,1024]{1,0:T(8,128)} %copy-done.4) | copy-start | bytes 3145732
  105.2 42.1 %all-to-all-start.1 = ((bf16[32,80,256]{2,1,0:T(8,128)(2,1)}), bf16[32,80,256]{2,1,0:T(8,128)(2,1)}, u32[]{:S(2)}, u32[]{:S(2)}) async-start(bf16[32,80,256]{2,1,0:T(8,128)(2,1)} %pad_maximum_fusion), calls=%async_computation.1 | async-start | bytes 2621440 | tf_op jit(solution)/shard_map/all_to_all | solution.py:93
  151.5 24.1 %all-to-all-start.2 = ((bf16[16,65,256]{2,1,0:T(8,128)(2,1)}), bf16[16,65,256]{2,1,0:T(8,128)(2,1)S(1)}, u32[]{:S(2)}, u32[]{:S(2)}) async-start(bf16[16,65,256]{2,1,0:T(8,128)(2,1)} %pad_maximum_fusion.1), calls=%async_computation.2 | async-start | bytes 1179648 | tf_op jit(solution)/shard_map/all_to_all | solution.py:106
  175.8 1.0 copy-start.1
  176.8 11.2 %copy-start.13 = (f32[64,256]{1,0:T(8,128)S(1)}, f32[64,256]{1,0:T(8,128)}, u32[]{:S(2)}) copy-start(f32[64,256]{1,0:T(8,128)} %param.11) | copy-start | bytes 196612
  177.7 26.3 %all-to-all-start.3 = ((f32[512,1,128]{2,1,0:T(1,128)}), f32[512,1,128]{2,1,0:T(1,128)S(1)}, u32[]{:S(2)}, u32[]{:S(2)}) async-start(f32[512,1,128]{2,1,0:T(1,128)} %broadcast_in_dim.39), calls=%async_computation.3 | async-start | bytes 524288 | tf_op jit(solution)/shard_map/all_to_all | solution.py:110
  186.7 1.3 copy-start.2
  206.2 1.0 copy-start.9
  206.2 1.5 copy-start.10
  206.2 1.5 copy-start.11
  206.2 1.5 copy-start.12

commit v4 on v3

--- a/solution.py
+++ b/solution.py
@@ -5,8 +5,9 @@
 
 
 def halve_lower(square):
-    lower = jnp.tril(square)
-    return lower - 0.5 * jnp.diag(jnp.diag(square))
+    row = lax.broadcasted_iota(jnp.int32, square.shape, 0)
+    col = lax.broadcasted_iota(jnp.int32, square.shape, 1)
+    return jnp.where(row > col, square, jnp.where(row == col, 0.5 * square, 0.0))
 
 
 def right_solve_t(factor, rhs):
@@ -75,11 +76,8 @@
     forward = jnp.dot(tile, panel_cols, preferred_element_type=jnp.float32)
     backward = inner_rows(tile, panel_rows)
     panel_exact = panel_own.astype(jnp.float32)
-    coupling_part = (
-        inner_rows(l21_bar, panel_exact, highest)
-        - inner_rows(forward, panel_rows.astype(jnp.float32), highest)
-        - inner_rows(backward, panel_cols.astype(jnp.float32), highest)
-    )
+    cross = inner_rows(panel_cols.astype(jnp.float32), backward, highest)
+    coupling_part = inner_rows(l21_bar, panel_exact, highest) - cross - cross.T
     high, low = split_pair(coupling_part)
     strip = width // n_col
     pieces = jnp.concatenate(
@@ -90,29 +88,31 @@
         ],
         axis=1,
     )
-    got = lax.all_to_all(pieces, "col", 0, 0, tiled=True).astype(jnp.float32)
-    row_share = got[:, :rows_own].sum(0)
-    coupling_col = (got[:, rows_own:rows_own + strip] + got[:, rows_own + strip:]).sum(0)
-    span = width // n_row
-    spread = coupling_col.reshape(strip, n_row, span).transpose(1, 0, 2).reshape(n_row, strip * span)
-    high, low = split_pair(spread)
+    got = lax.all_to_all(pieces, "col", 0, 0, tiled=True)
+    row_share = got[:, :rows_own].astype(jnp.float32).sum(0)
+    coupling_col = (
+        got[:, rows_own:rows_own + strip].astype(jnp.float32).sum(0)
+        + got[:, rows_own + strip:].astype(jnp.float32).sum(0)
+    )
+    span = strip * width // n_row
+    high, low = split_pair(coupling_col.reshape(n_row, span))
     pieces = jnp.concatenate(
         [
             backward.astype(jnp.bfloat16).reshape(n_row, rows_own, width),
-            jnp.concatenate([high, low], axis=1).reshape(n_row, 1, 2 * strip * span),
+            jnp.concatenate([high, low], axis=1).reshape(n_row, 1, 2 * span),
         ],
         axis=1,
     )
-    got = lax.all_to_all(pieces, "row", 0, 0, tiled=True).astype(jnp.float32)
-    col_share = got[:, :rows_own].sum(0)
-    mine = (got[:, rows_own, : strip * span] + got[:, rows_own, strip * span:]).sum(0)
+    got = lax.all_to_all(pieces, "row", 0, 0, tiled=True)
+    col_share = got[:, :rows_own].astype(jnp.float32).sum(0)
+    mine = (
+        got[:, rows_own, :span].astype(jnp.float32).sum(0)
+        + got[:, rows_own, span:].astype(jnp.float32).sum(0)
+    )
     n_all = n_row * n_col
-    blocks = lax.all_to_all(
-        jnp.broadcast_to(mine[None], (n_all, strip * span)), ("row", "col"), 0, 0, tiled=True
-    )
-    coupling = (
-        blocks.reshape(n_row, n_col, strip, span).transpose(1, 2, 0, 3).reshape(width, width)
-    )
+    coupling = lax.all_to_all(
+        jnp.broadcast_to(mine[None], (n_all, span)), ("col", "row"), 0, 0, tiled=True
+    ).reshape(width, width)
     trail = l21_bar - row_share - col_share
     a21_bar = jnp.dot(trail, inverse, precision=highest)
     l11_total = l11_bar - jnp.dot(inverse.T, coupling, precision=highest)

time: 213 us -> 201 us (0.944)
  local copies, waits for them, and re-layouts: 15.9 us -> 6.55 us
  other arithmetic: 53.1 us -> 50.3 us
    convert_element_type x3 -> x0, other arithmetic: 2.86 us -> none  [the longest x1 1.63 us: body(): got = lax.all_to_all(pieces, 'col', 0, 0, tiled=True).astype(jnp.float32)]
    transpose x2 -> x0, local copies, waits for them, and re-layouts: 2.47 us -> none  [the longest x1 1.82 us: body(): blocks.reshape(n_row, n_col, strip, span).transpose(1, 2, 0, 3)]
    gather x1 -> x0, local copies, waits for them, and re-layouts: 2.34 us -> none  [halve_lower(): return lower - 0.5 * jnp.diag(jnp.diag(square))]
    dot_general x4 -> x3, matrix products: 7.09 us -> 4.89 us  [inner_rows(): lax.dot_general(left, right, (((0,), (0,)), ((), ())), preferred_element_...]
    reshape x5 -> x2, local copies, waits for them, and re-layouts: 2.22 us -> 0.09 us  [the longest x1 0.07 us: body(): coupling = lax.all_to_all(jnp.broadcast_to(mine[None], (n_all, span)), ('...]
  transfers between devices with their start and end apart: 4 -> 4, of which waited for: 3 -> 3; matrix products, arithmetic and copies ran while one was open for 5% -> 4% of each run, Pallas kernels for 0% -> 0%
where the time goes in v4:
time: 201 us; the launch traced here: 200 us
  waiting for transfers between devices  67 us (33%)
  other arithmetic  50.3 us (25%)
  starting transfers between devices  34.4 us (17%)
  blocking collectives  25.4 us (13%)
  matrix products  15.8 us (8%)
  local copies, waits for them, and re-layouts  6.55 us (3%)
    all_to_all x1, waiting for transfers between devices, body(): got = lax.all_to_all(pieces, 'col', 0, 0, tiled=True)  32.2 us
    all_gather x1, blocking collectives, body(): panel_cols = lax.all_gather(panel_own, 'row', axis=0, tiled=True)  25.4 us
    another operation x4, other arithmetic, invert_lower(): return lax.linalg.triangular_solve(factor, eye, left_side=True, lower=True)  21.1 us
    all_to_all x1, waiting for transfers between devices, body(): got = lax.all_to_all(pieces, 'row', 0, 0, tiled=True)  18.6 us
    all_to_all x1, waiting for transfers between devices, body(): lax.all_to_all(jnp.broadcast_to(mine[None], (n_all, span)), ('col', 'row'...  16.1 us
    another operation x3, other arithmetic, factor_and_invert(): last = lax.linalg.cholesky(rest, symmetrize_input=False)  12.4 us
    another operation x3, other arithmetic, factor_and_invert(): first = lax.linalg.cholesky(square[:half, :half], symmetrize_input=False)  12.4 us
    all_to_all x1, starting transfers between devices, gather_rows(): lax.all_to_all(spread, axis, 0, 0, tiled=True).reshape(-1, part.shape[-1])  10.5 us
  transfers between devices with their start and end apart: 4, of which 3 were waited for; matrix products, arithmetic and copies ran while one was open for 4% of the time, Pallas kernels for 0%

profile of v4, /device:TPU:1, one launch (start us, length us, event | category | flops | bytes accessed | tf_op | source)
XLA Modules:
  0.0 200.3 jit_solution(10792857343647557424)
XLA Ops:
  0.6 0.9 slice.31
  1.5 11.7 %custom-call.8 = f32[128,128]{1,0:T(8,128)S(1)} custom-call(f32[128,128]{1,0:T(8,128)S(1)} %slice.31), custom_call_target="Cholesky" | custom-call | tf_op jit(solution)/shard_map/cholesky/custom-call.1 | solution.py:33
  14.6 9.8 %custom-call.9 = f32[1,128,128]{1,2,0:T(8,128)S(1)} custom-call(f32[1,128,128]{2,1,0:T(8,128)S(1)} %get-tuple-element.12), custom_call_target="InvertDiagBlocksLowerTriangular" | custom-call | tf_op jit(solution)/shard_map/triangular_solve/custom-call.0 | solution.py:27
  24.7 1.1 fusion.28
  25.8 1.1 convolution_subtract_fusion.1
  26.9 11.7 %custom-call.10 = f32[128,128]{1,0:T(8,128)S(1)} custom-call(f32[128,128]{1,0:T(8,128)S(1)} %convolution_subtract_fusion.1), custom_call_target="Cholesky" | custom-call | tf_op jit(solution)/shard_map/cholesky/custom-call.1 | solution.py:37
  40.0 10.0 %custom-call.11 = f32[1,128,128]{1,2,0:T(8,128)S(1)} custom-call(f32[1,128,128]{2,1,0:T(8,128)S(1)} %get-tuple-element.10), custom_call_target="InvertDiagBlocksLowerTriangular" | custom-call | tf_op jit(solution)/shard_map/triangular_solve/custom-call.0 | solution.py:27
  51.2 1.1 broadcast_in_dim.7
  52.3 10.5 %all-to-all-start = ((bf16[32,64,256]{2,1,0:T(8,128)(2,1)}), bf16[32,64,256]{2,1,0:T(8,128)(2,1)S(1)}, u32[]{:S(2)}, u32[]{:S(2)}) async-start(bf16[32,64,256]{2,1,0:T(8,128)(2,1)} %broadcast_in_dim.7), calls=%async_computation | async-start | bytes 2097152 | tf_op jit(solution)/shard_map/all_to_all | solution.py:55
  62.8 25.4 %all_gather.3 = bf16[1024,256]{1,0:T(8,128)(2,1)S(1)} all-gather(bf16[64,256]{1,0:T(8,128)(2,1)S(1)} %bitcast.65), channel_id=1, replica_groups=mesh['row'=16,'col'=32] {'row'}, dimensions={0}, use_global_device_ids=true | all-gather | bytes 557056 | tf_op jit(solution)/shard_map/all_gather | solution.py:75
  88.2 4.5 %fusion = bf16[2048,256]{0,1:T(8,128)(2,1)} fusion(bf16[1024,256]{1,0:T(8,128)(2,1)S(1)} %all_gather.3, bf16[2048,1024]{1,0:T(8,128)(2,1)} %bitcast.67), kind=kOutput, calls=%fused_computation.1 | convolution fusion | flops 1074266112 | bytes 5767168 | tf_op jit(solution)/shard_map/dot_general | solution.py:76
  92.7 1.5 copy.16
  94.2 1.0 copy-done.1
  95.2 3.8 %fusion.40 = f32[256,1024]{1,0:T(8,128)S(1)} fusion(bf16[2048,256]{1,0:T(8,128)(2,1)} %bitcast.63, bf16[2048,1024]{1,0:T(8,128)(2,1)} %bitcast.68), kind=kOutput, calls=%fused_computation.73 | convolution fusion | flops 1073741824 | bytes 6291456 | tf_op jit(solution)/shard_map/dot_general | solution.py:47
  100.3 1.2 pad_maximum_fusion
  101.4 9.5 %all-to-all-start.1 = ((bf16[32,80,256]{2,1,0:T(8,128)(2,1)}), bf16[32,80,256]{2,1,0:T(8,128)(2,1)S(1)}, u32[]{:S(2)}, u32[]{:S(2)}) async-start(bf16[32,80,256]{2,1,0:T(8,128)(2,1)} %pad_maximum_fusion), calls=%async_computation.1 | async-start | bytes 2621440 | tf_op jit(solution)/shard_map/all_to_all | solution.py:91
  111.2 32.2 %all-to-all-done.1 = bf16[32,80,256]{2,1,0:T(8,128)(2,1)S(1)} async-done(((bf16[32,80,256]{2,1,0:T(8,128)(2,1)}), bf16[32,80,256]{2,1,0:T(8,128)(2,1)S(1)}, u32[]{:S(2)}, u32[]{:S(2)}) %all-to-all-start.1) | async-done | bytes 1310752 | tf_op jit(solution)/shard_map/all_to_all | solution.py:91
  143.5 0.9 pad_maximum_fusion.1
  144.4 5.4 %all-to-all-start.2 = ((bf16[16,65,256]{2,1,0:T(8,128)(2,1)}), bf16[16,65,256]{2,1,0:T(8,128)(2,1)S(1)}, u32[]{:S(2)}, u32[]{:S(2)}) async-start(bf16[16,65,256]{2,1,0:T(8,128)(2,1)} %pad_maximum_fusion.1), calls=%async_computation.2 | async-start | bytes 1179648 | tf_op jit(solution)/shard_map/all_to_all | solution.py:106
  149.9 18.6 %all-to-all-done.2 = bf16[16,65,256]{2,1,0:T(8,128)(2,1)S(1)} async-done(((bf16[16,65,256]{2,1,0:T(8,128)(2,1)}), bf16[16,65,256]{2,1,0:T(8,128)(2,1)S(1)}, u32[]{:S(2)}, u32[]{:S(2)}) %all-to-all-start.2) | async-done | bytes 532512 | tf_op jit(solution)/shard_map/all_to_all | solution.py:106
  169.4 9.0 %all-to-all-start.3 = ((f32[512,1,128]{2,1,0:T(1,128)}), f32[512,1,128]{2,1,0:T(1,128)S(1)}, u32[]{:S(2)}, u32[]{:S(2)}) async-start(f32[512,1,128]{2,1,0:T(1,128)} %broadcast_in_dim.8), calls=%async_computation.3 | async-start | bytes 524288 | tf_op jit(solution)/shard_map/all_to_all | solution.py:113
  178.6 0.9 fusion.25
  179.5 16.1 %all-to-all-done.3 = f32[512,1,128]{2,1,0:T(1,128)S(1)} async-done(((f32[512,1,128]{2,1,0:T(1,128)}), f32[512,1,128]{2,1,0:T(1,128)S(1)}, u32[]{:S(2)}, u32[]{:S(2)}) %all-to-all-start.3) | async-done | bytes 262176 | tf_op jit(solution)/shard_map/all_to_all | solution.py:113
  196.2 1.3 reduce.29
  (45 shorter events, 10.3 us)
Async XLA Ops:
  0.6 50.2 %copy-start = (f32[64,256]{1,0:T(8,128)S(1)}, f32[64,256]{1,0:T(8,128)}, u32[]{:S(2)}) copy-start(f32[64,256]{1,0:T(8,128)} %param.10) | copy-start | bytes 196612
  52.3 41.9 %all-to-all-start = ((bf16[32,64,256]{2,1,0:T(8,128)(2,1)}), bf16[32,64,256]{2,1,0:T(8,128)(2,1)S(1)}, u32[]{:S(2)}, u32[]{:S(2)}) async-start(bf16[32,64,256]{2,1,0:T(8,128)(2,1)} %broadcast_in_dim.7), calls=%async_computation | async-start | bytes 2097152 | tf_op jit(solution)/shard_map/all_to_all | solution.py:55
  94.2 1.0 copy-start.1
  99.0 0.9 copy-start.3
  101.4 42.0 %all-to-all-start.1 = ((bf16[32,80,256]{2,1,0:T(8,128)(2,1)}), bf16[32,80,256]{2,1,0:T(8,128)(2,1)S(1)}, u32[]{:S(2)}, u32[]{:S(2)}) async-start(bf16[32,80,256]{2,1,0:T(8,128)(2,1)} %pad_maximum_fusion), calls=%async_computation.1 | async-start | bytes 2621440 | tf_op jit(solution)/shard_map/all_to_all | solution.py:91
  144.4 24.1 %all-to-all-start.2 = ((bf16[16,65,256]{2,1,0:T(8,128)(2,1)}), bf16[16,65,256]{2,1,0:T(8,128)(2,1)S(1)}, u32[]{:S(2)}, u32[]{:S(2)}) async-start(bf16[16,65,256]{2,1,0:T(8,128)(2,1)} %pad_maximum_fusion.1), calls=%async_computation.2 | async-start | bytes 1179648 | tf_op jit(solution)/shard_map/all_to_all | solution.py:106
  149.8 47.7 %copy-start.2 = (f32[256,256]{1,0:T(8,128)S(1)}, f32[256,256]{1,0:T(8,128)}, u32[]{:S(2)}) copy-start(f32[256,256]{1,0:T(8,128)} %param.9) | copy-start | bytes 786436
  169.4 26.3 %all-to-all-start.3 = ((f32[512,1,128]{2,1,0:T(1,128)}), f32[512,1,128]{2,1,0:T(1,128)S(1)}, u32[]{:S(2)}, u32[]{:S(2)}) async-start(f32[512,1,128]{2,1,0:T(1,128)} %broadcast_in_dim.8), calls=%async_computation.3 | async-start | bytes 524288 | tf_op jit(solution)/shard_map/all_to_all | solution.py:113

commit v5 on v4

--- a/solution.py
+++ b/solution.py
@@ -68,10 +68,11 @@
     rows_own, width = a21.shape
     blocks_here = s_bar.shape[0]
     tile = s_bar.reshape(blocks_here * rows_own, s_bar.shape[3])
+    a21_rows = gather_rows(a21, "col", n_col)
     l11, inverse = factor_and_invert(a11)
     l21_own = jnp.dot(a21, inverse.T, precision=highest)
     panel_own = l21_own.astype(jnp.bfloat16)
-    panel_rows = gather_rows(panel_own, "col", n_col)
+    panel_rows = jnp.dot(a21_rows, inverse.T, precision=highest).astype(jnp.bfloat16)
     panel_cols = lax.all_gather(panel_own, "row", axis=0, tiled=True)
     forward = jnp.dot(tile, panel_cols, preferred_element_type=jnp.float32)
     backward = inner_rows(tile, panel_rows)

time: 201 us -> 203 us (level)
  transfers between devices with their start and end apart: 4 -> 4, of which waited for: 3 -> 3; matrix products, arithmetic and copies ran while one was open for 4% -> 28% of each run, Pallas kernels for 0% -> 0%
where the time goes in v5:
time: 203 us
  waiting for transfers between devices  66.9 us (33%)
  other arithmetic  51.5 us (25%)
  starting transfers between devices  34.7 us (17%)
  blocking collectives  25.4 us (13%)
  matrix products  15.8 us (8%)
  local copies, waits for them, and re-layouts  7.45 us (4%)
    all_to_all x1, waiting for transfers between devices, body(): got = lax.all_to_all(pieces, 'col', 0, 0, tiled=True)  32.2 us
    all_gather x1, blocking collectives, body(): panel_cols = lax.all_gather(panel_own, 'row', axis=0, tiled=True)  25.4 us
    another operation x4, other arithmetic, invert_lower(): return lax.linalg.triangular_solve(factor, eye, left_side=True, lower=True)  22.3 us
    all_to_all x1, waiting for transfers between devices, body(): got = lax.all_to_all(pieces, 'row', 0, 0, tiled=True)  18.6 us
    all_to_all x1, waiting for transfers between devices, body(): lax.all_to_all(jnp.broadcast_to(mine[None], (n_all, span)), ('col', 'row'...  16.1 us
    another operation x3, other arithmetic, factor_and_invert(): last = lax.linalg.cholesky(rest, symmetrize_input=False)  12.4 us
    another operation x3, other arithmetic, factor_and_invert(): first = lax.linalg.cholesky(square[:half, :half], symmetrize_input=False)  12.4 us
    all_to_all x1, starting transfers between devices, gather_rows(): lax.all_to_all(spread, axis, 0, 0, tiled=True).reshape(-1, part.shape[-1])  10.6 us
  transfers between devices with their start and end apart: 4, of which 3 were waited for; matrix products, arithmetic and copies ran while one was open for 28% of the time, Pallas kernels for 0%

profile of v5, /device:TPU:1, one launch (start us, length us, event | category | flops | bytes accessed | tf_op | source)
XLA Modules:
  0.0 202.7 jit_solution(11729378472679310710)
XLA Ops:
  0.6 2.4 %broadcast_in_dim.7 = f32[32,64,256]{2,1,0:T(8,128)} broadcast(f32[64,256]{1,0:T(8,128)} %param.10), dimensions={1,2} | broadcast | bytes 2162688 | tf_op jit(solution)/shard_map/broadcast_in_dim | solution.py:54
  3.1 10.6 %all-to-all-start = ((f32[32,64,256]{2,1,0:T(8,128)}), f32[32,64,256]{2,1,0:T(8,128)S(1)}, u32[]{:S(2)}, u32[]{:S(2)}) async-start(f32[32,64,256]{2,1,0:T(8,128)} %broadcast_in_dim.7), calls=%async_computation | async-start | bytes 4194304 | tf_op jit(solution)/shard_map/all_to_all | solution.py:55
  13.7 11.7 %custom-call.8 = f32[128,128]{1,0:T(8,128)S(1)} custom-call(f32[128,128]{1,0:T(8,128)S(1)} %slice.31), custom_call_target="Cholesky" | custom-call | tf_op jit(solution)/shard_map/cholesky/custom-call.1 | solution.py:33
  26.1 1.3 select_bitcast_fusion.1
  27.4 9.8 %custom-call.9 = f32[1,128,128]{1,2,0:T(8,128)S(1)} custom-call(f32[1,128,128]{2,1,0:T(8,128)S(1)} %get-tuple-element.12), custom_call_target="InvertDiagBlocksLowerTriangular" | custom-call | tf_op jit(solution)/shard_map/triangular_solve/custom-call.0 | solution.py:27
  38.0 11.7 %custom-call.10 = f32[128,128]{1,0:T(8,128)S(1)} custom-call(f32[128,128]{1,0:T(8,128)S(1)} %convolution_subtract_fusion.1), custom_call_target="Cholesky" | custom-call | tf_op jit(solution)/shard_map/cholesky/custom-call.1 | solution.py:37
  50.4 1.3 select_bitcast_fusion
  51.7 10.0 %custom-call.11 = f32[1,128,128]{1,2,0:T(8,128)S(1)} custom-call(f32[1,128,128]{2,1,0:T(8,128)S(1)} %get-tuple-element.10), custom_call_target="InvertDiagBlocksLowerTriangular" | custom-call | tf_op jit(solution)/shard_map/triangular_solve/custom-call.0 | solution.py:27
  63.6 25.4 %all_gather.3 = bf16[1024,256]{1,0:T(8,128)(2,1)S(1)} all-gather(bf16[64,256]{1,0:T(8,128)(2,1)S(1)} %bitcast.66), channel_id=1, replica_groups=mesh['row'=16,'col'=32] {'row'}, dimensions={0}, use_global_device_ids=true | all-gather | bytes 557056 | tf_op jit(solution)/shard_map/all_gather | solution.py:76
  89.7 4.5 %fusion = bf16[2048,256]{0,1:T(8,128)(2,1)} fusion(bf16[1024,256]{1,0:T(8,128)(2,1)S(1)} %all_gather.3, bf16[2048,1024]{1,0:T(8,128)(2,1)} %bitcast.67), kind=kOutput, calls=%fused_computation.2 | convolution fusion | flops 1074266112 | bytes 5767168 | tf_op jit(solution)/shard_map/dot_general | solution.py:77
  94.2 1.5 copy.16
  95.7 1.9 convolution_convert_fusion
  97.7 3.5 %fusion.40 = f32[256,1024]{1,0:T(8,128)S(1)} fusion(bf16[256,2048]{1,0:T(8,128)(2,1)S(1)} %convolution_convert_fusion, bf16[2048,1024]{1,0:T(8,128)(2,1)} %bitcast.68), kind=kOutput, calls=%fused_computation.74 | convolution fusion | flops 1073741824 | bytes 6291456 | tf_op jit(solution)/shard_map/dot_general | solution.py:47
  102.5 1.2 pad_maximum_fusion
  103.7 9.5 %all-to-all-start.1 = ((bf16[32,80,256]{2,1,0:T(8,128)(2,1)}), bf16[32,80,256]{2,1,0:T(8,128)(2,1)S(1)}, u32[]{:S(2)}, u32[]{:S(2)}) async-start(bf16[32,80,256]{2,1,0:T(8,128)(2,1)} %pad_maximum_fusion), calls=%async_computation.1 | async-start | bytes 2621440 | tf_op jit(solution)/shard_map/all_to_all | solution.py:92
  113.4 32.2 %all-to-all-done.1 = bf16[32,80,256]{2,1,0:T(8,128)(2,1)S(1)} async-done(((bf16[32,80,256]{2,1,0:T(8,128)(2,1)}), bf16[32,80,256]{2,1,0:T(8,128)(2,1)S(1)}, u32[]{:S(2)}, u32[]{:S(2)}) %all-to-all-start.1) | async-done | bytes 1310752 | tf_op jit(solution)/shard_map/all_to_all | solution.py:92
  145.8 0.9 pad_maximum_fusion.1
  146.6 5.5 %all-to-all-start.2 = ((bf16[16,65,256]{2,1,0:T(8,128)(2,1)}), bf16[16,65,256]{2,1,0:T(8,128)(2,1)S(1)}, u32[]{:S(2)}, u32[]{:S(2)}) async-start(bf16[16,65,256]{2,1,0:T(8,128)(2,1)} %pad_maximum_fusion.1), calls=%async_computation.2 | async-start | bytes 1179648 | tf_op jit(solution)/shard_map/all_to_all | solution.py:107
  152.3 18.6 %all-to-all-done.2 = bf16[16,65,256]{2,1,0:T(8,128)(2,1)S(1)} async-done(((bf16[16,65,256]{2,1,0:T(8,128)(2,1)}), bf16[16,65,256]{2,1,0:T(8,128)(2,1)S(1)}, u32[]{:S(2)}, u32[]{:S(2)}) %all-to-all-start.2) | async-done | bytes 532512 | tf_op jit(solution)/shard_map/all_to_all | solution.py:107
  170.9 0.8 broadcast_in_dim.8
  171.8 9.0 %all-to-all-start.3 = ((f32[512,1,128]{2,1,0:T(1,128)}), f32[512,1,128]{2,1,0:T(1,128)S(1)}, u32[]{:S(2)}, u32[]{:S(2)}) async-start(f32[512,1,128]{2,1,0:T(1,128)} %broadcast_in_dim.8), calls=%async_computation.3 | async-start | bytes 524288 | tf_op jit(solution)/shard_map/all_to_all | solution.py:114
  181.1 0.9 fusion.25
  182.0 16.1 %all-to-all-done.3 = f32[512,1,128]{2,1,0:T(1,128)S(1)} async-done(((f32[512,1,128]{2,1,0:T(1,128)}), f32[512,1,128]{2,1,0:T(1,128)S(1)}, u32[]{:S(2)}, u32[]{:S(2)}) %all-to-all-start.3) | async-done | bytes 262176 | tf_op jit(solution)/shard_map/all_to_all | solution.py:114
  198.6 1.3 reduce.29
  (68 shorter events, 10.1 us)
Async XLA Ops:
  3.1 10.6 %copy-start.9 = (f32[256,256]{1,0:T(8,128)S(1)}, f32[256,256]{1,0:T(8,128)}, u32[]{:S(2)}) copy-start(f32[256,256]{1,0:T(8,128)} %param.8) | copy-start | bytes 786436
  3.1 59.5 %copy-start.12 = (f32[64,256]{1,0:T(8,128)S(1)}, f32[64,256]{1,0:T(8,128)}, u32[]{:S(2)}) copy-start(f32[64,256]{1,0:T(8,128)} %param.10) | copy-start | bytes 196612
  3.1 92.6 %all-to-all-start = ((f32[32,64,256]{2,1,0:T(8,128)}), f32[32,64,256]{2,1,0:T(8,128)S(1)}, u32[]{:S(2)}, u32[]{:S(2)}) async-start(f32[32,64,256]{2,1,0:T(8,128)} %broadcast_in_dim.7), calls=%async_computation | async-start | bytes 4194304 | tf_op jit(solution)/shard_map/all_to_all | solution.py:55
  62.0 33.6 %copy-start.4 = (f32[128,128]{1,0:T(8,128)}, f32[128,128]{1,0:T(8,128)S(1)}, u32[]{:S(2)}) copy-start(f32[128,128]{1,0:T(8,128)S(1)} %copy.15) | copy-start | bytes 196612
  62.6 33.1 %copy-start.2 = (f32[128,128]{1,0:T(8,128)}, f32[128,128]{1,0:T(8,128)S(1)}, u32[]{:S(2)}) copy-start(f32[128,128]{1,0:T(8,128)S(1)} %convolution_negate_fusion) | copy-start | bytes 196612
  62.9 0.6 copy-start.10
  88.9 0.8 copy-start
  97.6 3.5 %copy-start.1 = (bf16[1024,256]{1,0:T(8,128)(2,1)S(1)}, bf16[1024,256]{1,0:T(8,128)(2,1)}, u32[]{:S(2)}) copy-start(bf16[1024,256]{1,0:T(8,128)(2,1)} %copy-done) | copy-start | bytes 1572868
  101.2 0.9 copy-start.11
  101.2 0.9 copy-start.13
  103.7 42.0 %all-to-all-start.1 = ((bf16[32,80,256]{2,1,0:T(8,128)(2,1)}), bf16[32,80,256]{2,1,0:T(8,128)(2,1)S(1)}, u32[]{:S(2)}, u32[]{:S(2)}) async-start(bf16[32,80,256]{2,1,0:T(8,128)(2,1)} %pad_maximum_fusion), calls=%async_computation.1 | async-start | bytes 2621440 | tf_op jit(solution)/shard_map/all_to_all | solution.py:92
  146.6 34.4 %copy-start.3 = (f32[128,128]{1,0:T(8,128)S(1)}, f32[128,128]{1,0:T(8,128)}, u32[]{:S(2)}) copy-start(f32[128,128]{1,0:T(8,128)} %copy-done.2) | copy-start | bytes 196612
  146.6 34.4 %copy-start.5 = (f32[128,128]{1,0:T(8,128)S(1)}, f32[128,128]{1,0:T(8,128)}, u32[]{:S(2)}) copy-start(f32[128,128]{1,0:T(8,128)} %copy-done.4) | copy-start | bytes 196612
  146.6 34.4 %copy-start.14 = (f32[64,256]{1,0:T(8,128)S(1)}, f32[64,256]{1,0:T(8,128)}, u32[]{:S(2)}) copy-start(f32[64,256]{1,0:T(8,128)} %param.11) | copy-start | bytes 196612
  146.6 24.2 %all-to-all-start.2 = ((bf16[16,65,256]{2,1,0:T(8,128)(2,1)}), bf16[16,65,256]{2,1,0:T(8,128)(2,1)S(1)}, u32[]{:S(2)}, u32[]{:S(2)}) async-start(bf16[16,65,256]{2,1,0:T(8,128)(2,1)} %pad_maximum_fusion.1), calls=%async_computation.2 | async-start | bytes 1179648 | tf_op jit(solution)/shard_map/all_to_all | solution.py:107
  152.2 47.7 %copy-start.6 = (f32[256,256]{1,0:T(8,128)S(1)}, f32[256,256]{1,0:T(8,128)}, u32[]{:S(2)}) copy-start(f32[256,256]{1,0:T(8,128)} %param.9) | copy-start | bytes 786436
  171.8 26.3 %all-to-all-start.3 = ((f32[512,1,128]{2,1,0:T(1,128)}), f32[512,1,128]{2,1,0:T(1,128)S(1)}, u32[]{:S(2)}, u32[]{:S(2)}) async-start(f32[512,1,128]{2,1,0:T(1,128)} %broadcast_in_dim.8), calls=%async_computation.3 | async-start | bytes 524288 | tf_op jit(solution)/shard_map/all_to_all | solution.py:114
  180.8 19.7 %copy-start.7 = (f32[128,128]{1,0:T(8,128)S(1)}, f32[128,128]{1,0:T(8,128)}, u32[]{:S(2)}) copy-start(f32[128,128]{1,0:T(8,128)} %get-tuple-element.13) | copy-start | bytes 196612
  180.8 19.7 %copy-start.8 = (f32[128,128]{1,0:T(8,128)S(1)}, f32[128,128]{1,0:T(8,128)}, u32[]{:S(2)}) copy-start(f32[128,128]{1,0:T(8,128)} %get-tuple-element.11) | copy-start | bytes 196612

commit v6 on v4

--- a/solution.py
+++ b/solution.py
@@ -79,39 +79,39 @@
     cross = inner_rows(panel_cols.astype(jnp.float32), backward, highest)
     coupling_part = inner_rows(l21_bar, panel_exact, highest) - cross - cross.T
     high, low = split_pair(coupling_part)
-    strip = width // n_col
+    strip = width // n_row
+    pieces = jnp.concatenate(
+        [
+            backward.astype(jnp.bfloat16).reshape(n_row, rows_own, width),
+            high.reshape(n_row, strip, width),
+            low.reshape(n_row, strip, width),
+        ],
+        axis=1,
+    )
+    got = lax.all_to_all(pieces, "row", 0, 0, tiled=True)
+    col_share = got[:, :rows_own].astype(jnp.float32).sum(0)
+    coupling_row = (
+        got[:, rows_own:rows_own + strip].astype(jnp.float32).sum(0)
+        + got[:, rows_own + strip:].astype(jnp.float32).sum(0)
+    )
+    span = strip * width // n_col
+    high, low = split_pair(coupling_row.reshape(n_col, span))
     pieces = jnp.concatenate(
         [
             forward.astype(jnp.bfloat16).reshape(n_col, rows_own, width),
-            high.reshape(n_col, strip, width),
-            low.reshape(n_col, strip, width),
+            jnp.concatenate([high, low], axis=1).reshape(n_col, 1, 2 * span),
         ],
         axis=1,
     )
     got = lax.all_to_all(pieces, "col", 0, 0, tiled=True)
     row_share = got[:, :rows_own].astype(jnp.float32).sum(0)
-    coupling_col = (
-        got[:, rows_own:rows_own + strip].astype(jnp.float32).sum(0)
-        + got[:, rows_own + strip:].astype(jnp.float32).sum(0)
-    )
-    span = strip * width // n_row
-    high, low = split_pair(coupling_col.reshape(n_row, span))
-    pieces = jnp.concatenate(
-        [
-            backward.astype(jnp.bfloat16).reshape(n_row, rows_own, width),
-            jnp.concatenate([high, low], axis=1).reshape(n_row, 1, 2 * span),
-        ],
-        axis=1,
-    )
-    got = lax.all_to_all(pieces, "row", 0, 0, tiled=True)
-    col_share = got[:, :rows_own].astype(jnp.float32).sum(0)
     mine = (
         got[:, rows_own, :span].astype(jnp.float32).sum(0)
         + got[:, rows_own, span:].astype(jnp.float32).sum(0)
     )
     n_all = n_row * n_col
     coupling = lax.all_to_all(
-        jnp.broadcast_to(mine[None], (n_all, span)), ("col", "row"), 0, 0, tiled=True
+        jnp.broadcast_to(mine[None], (n_all, span)), ("row", "col"), 0, 0, tiled=True
     ).reshape(width, width)
     trail = l21_bar - row_share - col_share
     a21_bar = jnp.dot(trail, inverse, precision=highest)

time: 201 us -> 201 us (level)
  starting transfers between devices: 34.4 us -> 39.9 us
    all_to_all x1, starting transfers between devices: 5.4 us -> 13.1 us  [body(): got = lax.all_to_all(pieces, 'row', 0, 0, tiled=True)]
    all_to_all x1, starting transfers between devices: 9.5 us -> 5.3 us  [body(): got = lax.all_to_all(pieces, 'col', 0, 0, tiled=True)]
    all_to_all x1, waiting for transfers between devices: 32.2 us -> 29.4 us  [body(): got = lax.all_to_all(pieces, 'col', 0, 0, tiled=True)]
  transfers between devices with their start and end apart: 4 -> 4, of which waited for: 3 -> 4; matrix products, arithmetic and copies ran while one was open for 4% -> 3% of each run, Pallas kernels for 0% -> 0%
where the time goes in v6:
time: 201 us
  waiting for transfers between devices  65 us (32%)
  other arithmetic  50.3 us (25%)
  starting transfers between devices  39.9 us (20%)
  blocking collectives  25.4 us (13%)
  matrix products  14.5 us (7%)
  local copies, waits for them, and re-layouts  4.63 us (2%)
    all_to_all x1, waiting for transfers between devices, body(): got = lax.all_to_all(pieces, 'col', 0, 0, tiled=True)  29.4 us
    all_gather x1, blocking collectives, body(): panel_cols = lax.all_gather(panel_own, 'row', axis=0, tiled=True)  25.4 us
    another operation x4, other arithmetic, invert_lower(): return lax.linalg.triangular_solve(factor, eye, left_side=True, lower=True)  21.1 us
    all_to_all x1, waiting for transfers between devices, body(): got = lax.all_to_all(pieces, 'row', 0, 0, tiled=True)  18.7 us
    all_to_all x1, waiting for transfers between devices, body(): lax.all_to_all(jnp.broadcast_to(mine[None], (n_all, span)), ('row', 'col'...  16.1 us
    all_to_all x1, starting transfers between devices, body(): got = lax.all_to_all(pieces, 'row', 0, 0, tiled=True)  13.1 us
    another operation x3, other arithmetic, factor_and_invert(): last = lax.linalg.cholesky(rest, symmetrize_input=False)  12.4 us
    another operation x3, other arithmetic, factor_and_invert(): first = lax.linalg.cholesky(square[:half, :half], symmetrize_input=False)  12.4 us
  transfers between devices with their start and end apart: 4, of which 4 were waited for; matrix products, arithmetic and copies ran while one was open for 3% of the time, Pallas kernels for 0%

profile of v6, /device:TPU:1, one launch (start us, length us, event | category | flops | bytes accessed | tf_op | source)
XLA Modules:
  0.0 200.7 jit_solution(2661141951581157364)
XLA Ops:
  0.6 0.9 slice.31
  1.5 11.7 %custom-call.8 = f32[128,128]{1,0:T(8,128)S(1)} custom-call(f32[128,128]{1,0:T(8,128)S(1)} %slice.31), custom_call_target="Cholesky" | custom-call | tf_op jit(solution)/shard_map/cholesky/custom-call.1 | solution.py:33
  14.6 9.8 %custom-call.9 = f32[1,128,128]{1,2,0:T(8,128)S(1)} custom-call(f32[1,128,128]{2,1,0:T(8,128)S(1)} %get-tuple-element.14), custom_call_target="InvertDiagBlocksLowerTriangular" | custom-call | tf_op jit(solution)/shard_map/triangular_solve/custom-call.0 | solution.py:27
  24.7 1.1 fusion.27
  25.8 1.1 convolution_subtract_fusion.1
  26.9 11.7 %custom-call.10 = f32[128,128]{1,0:T(8,128)S(1)} custom-call(f32[128,128]{1,0:T(8,128)S(1)} %convolution_subtract_fusion.1), custom_call_target="Cholesky" | custom-call | tf_op jit(solution)/shard_map/cholesky/custom-call.1 | solution.py:37
  40.0 10.0 %custom-call.11 = f32[1,128,128]{1,2,0:T(8,128)S(1)} custom-call(f32[1,128,128]{2,1,0:T(8,128)S(1)} %get-tuple-element.12), custom_call_target="InvertDiagBlocksLowerTriangular" | custom-call | tf_op jit(solution)/shard_map/triangular_solve/custom-call.0 | solution.py:27
  51.2 1.1 broadcast_in_dim.7
  52.3 10.5 %all-to-all-start = ((bf16[32,64,256]{2,1,0:T(8,128)(2,1)}), bf16[32,64,256]{2,1,0:T(8,128)(2,1)S(1)}, u32[]{:S(2)}, u32[]{:S(2)}) async-start(bf16[32,64,256]{2,1,0:T(8,128)(2,1)} %broadcast_in_dim.7), calls=%async_computation | async-start | bytes 2097152 | tf_op jit(solution)/shard_map/all_to_all | solution.py:55
  62.8 25.4 %all_gather.3 = bf16[1024,256]{1,0:T(8,128)(2,1)S(1)} all-gather(bf16[64,256]{1,0:T(8,128)(2,1)S(1)} %bitcast.61), channel_id=1, replica_groups=mesh['row'=16,'col'=32] {'row'}, dimensions={0}, use_global_device_ids=true | all-gather | bytes 557056 | tf_op jit(solution)/shard_map/all_gather | solution.py:75
  88.2 0.8 all-to-all-done
  89.0 3.5 %fusion.39 = f32[256,1024]{1,0:T(8,128)S(1)} fusion(bf16[2048,256]{1,0:T(8,128)(2,1)S(1)} %bitcast.57, bf16[2048,1024]{1,0:T(8,128)(2,1)} %bitcast.63), kind=kOutput, calls=%fused_computation.71 | convolution fusion | flops 1073741824 | bytes 6291456 | tf_op jit(solution)/shard_map/dot_general | solution.py:47
  94.0 0.9 pad_maximum_fusion.1
  95.0 13.1 %all-to-all-start.1 = ((bf16[16,96,256]{2,1,0:T(8,128)(2,1)}), bf16[16,96,256]{2,1,0:T(8,128)(2,1)S(1)}, u32[]{:S(2)}, u32[]{:S(2)}) async-start(bf16[16,96,256]{2,1,0:T(8,128)(2,1)} %pad_maximum_fusion.1), calls=%async_computation.1 | async-start | bytes 1572864 | tf_op jit(solution)/shard_map/all_to_all | solution.py:91
  108.1 3.5 %fusion = bf16[2048,256]{0,1:T(8,128)(2,1)S(1)} fusion(bf16[1024,256]{1,0:T(8,128)(2,1)S(1)} %all_gather.3, bf16[2048,1024]{1,0:T(8,128)(2,1)} %bitcast.64), kind=kOutput, calls=%fused_computation.1 | convolution fusion | flops 1074266112 | bytes 5767168 | tf_op jit(solution)/shard_map/dot_general | solution.py:76
  112.1 18.7 %all-to-all-done.1 = bf16[16,96,256]{2,1,0:T(8,128)(2,1)S(1)} async-done(((bf16[16,96,256]{2,1,0:T(8,128)(2,1)}), bf16[16,96,256]{2,1,0:T(8,128)(2,1)S(1)}, u32[]{:S(2)}, u32[]{:S(2)}) %all-to-all-start.1) | async-done | bytes 786464 | tf_op jit(solution)/shard_map/all_to_all | solution.py:91
  131.0 1.1 pad_maximum_fusion
  132.1 5.3 %all-to-all-start.2 = ((bf16[32,65,256]{2,1,0:T(8,128)(2,1)}), bf16[32,65,256]{2,1,0:T(8,128)(2,1)S(1)}, u32[]{:S(2)}, u32[]{:S(2)}) async-start(bf16[32,65,256]{2,1,0:T(8,128)(2,1)} %pad_maximum_fusion), calls=%async_computation.2 | async-start | bytes 2359296 | tf_op jit(solution)/shard_map/all_to_all | solution.py:106
  137.5 29.4 %all-to-all-done.2 = bf16[32,65,256]{2,1,0:T(8,128)(2,1)S(1)} async-done(((bf16[32,65,256]{2,1,0:T(8,128)(2,1)}), bf16[32,65,256]{2,1,0:T(8,128)(2,1)S(1)}, u32[]{:S(2)}, u32[]{:S(2)}) %all-to-all-start.2) | async-done | bytes 1064992 | tf_op jit(solution)/shard_map/all_to_all | solution.py:106
  167.0 0.8 broadcast_in_dim.8
  167.8 11.0 %all-to-all-start.3 = ((f32[512,1,128]{2,1,0:T(1,128)}), f32[512,1,128]{2,1,0:T(1,128)S(1)}, u32[]{:S(2)}, u32[]{:S(2)}) async-start(f32[512,1,128]{2,1,0:T(1,128)} %broadcast_in_dim.8), calls=%async_computation.3 | async-start | bytes 524288 | tf_op jit(solution)/shard_map/all_to_all | solution.py:113
  179.0 0.9 fusion.24
  179.9 16.1 %all-to-all-done.3 = f32[512,1,128]{2,1,0:T(1,128)S(1)} async-done(((f32[512,1,128]{2,1,0:T(1,128)}), f32[512,1,128]{2,1,0:T(1,128)S(1)}, u32[]{:S(2)}, u32[]{:S(2)}) %all-to-all-start.3) | async-done | bytes 262176 | tf_op jit(solution)/shard_map/all_to_all | solution.py:113
  196.6 1.3 reduce.29
  (43 shorter events, 10.0 us)
Async XLA Ops:
  0.6 50.2 %copy-start = (f32[64,256]{1,0:T(8,128)S(1)}, f32[64,256]{1,0:T(8,128)}, u32[]{:S(2)}) copy-start(f32[64,256]{1,0:T(8,128)} %param.10) | copy-start | bytes 196612
  52.3 36.7 %all-to-all-start = ((bf16[32,64,256]{2,1,0:T(8,128)(2,1)}), bf16[32,64,256]{2,1,0:T(8,128)(2,1)S(1)}, u32[]{:S(2)}, u32[]{:S(2)}) async-start(bf16[32,64,256]{2,1,0:T(8,128)(2,1)} %broadcast_in_dim.7), calls=%async_computation | async-start | bytes 2097152 | tf_op jit(solution)/shard_map/all_to_all | solution.py:55
  92.5 1.1 copy-start.2
  95.0 35.9 %all-to-all-start.1 = ((bf16[16,96,256]{2,1,0:T(8,128)(2,1)}), bf16[16,96,256]{2,1,0:T(8,128)(2,1)S(1)}, u32[]{:S(2)}, u32[]{:S(2)}) async-start(bf16[16,96,256]{2,1,0:T(8,128)(2,1)} %pad_maximum_fusion.1), calls=%async_computation.1 | async-start | bytes 1572864 | tf_op jit(solution)/shard_map/all_to_all | solution.py:91
  132.1 34.8 %all-to-all-start.2 = ((bf16[32,65,256]{2,1,0:T(8,128)(2,1)}), bf16[32,65,256]{2,1,0:T(8,128)(2,1)S(1)}, u32[]{:S(2)}, u32[]{:S(2)}) async-start(bf16[32,65,256]{2,1,0:T(8,128)(2,1)} %pad_maximum_fusion), calls=%async_computation.2 | async-start | bytes 2359296 | tf_op jit(solution)/shard_map/all_to_all | solution.py:106
  137.4 60.5 %copy-start.1 = (f32[256,256]{1,0:T(8,128)S(1)}, f32[256,256]{1,0:T(8,128)}, u32[]{:S(2)}) copy-start(f32[256,256]{1,0:T(8,128)} %param.9) | copy-start | bytes 786436
  167.8 28.2 %all-to-all-start.3 = ((f32[512,1,128]{2,1,0:T(1,128)}), f32[512,1,128]{2,1,0:T(1,128)S(1)}, u32[]{:S(2)}, u32[]{:S(2)}) async-start(f32[512,1,128]{2,1,0:T(1,128)} %broadcast_in_dim.8), calls=%async_computation.3 | async-start | bytes 524288 | tf_op jit(solution)/shard_map/all_to_all | solution.py:113

commit v7 on v4

--- a/solution.py
+++ b/solution.py
@@ -94,24 +94,13 @@
         got[:, rows_own:rows_own + strip].astype(jnp.float32).sum(0)
         + got[:, rows_own + strip:].astype(jnp.float32).sum(0)
     )
-    span = strip * width // n_row
-    high, low = split_pair(coupling_col.reshape(n_row, span))
-    pieces = jnp.concatenate(
-        [
-            backward.astype(jnp.bfloat16).reshape(n_row, rows_own, width),
-            jnp.concatenate([high, low], axis=1).reshape(n_row, 1, 2 * span),
-        ],
-        axis=1,
+    got = lax.all_to_all(
+        backward.astype(jnp.bfloat16).reshape(n_row, rows_own, width), "row", 0, 0, tiled=True
     )
-    got = lax.all_to_all(pieces, "row", 0, 0, tiled=True)
-    col_share = got[:, :rows_own].astype(jnp.float32).sum(0)
-    mine = (
-        got[:, rows_own, :span].astype(jnp.float32).sum(0)
-        + got[:, rows_own, span:].astype(jnp.float32).sum(0)
-    )
-    n_all = n_row * n_col
+    col_share = got.astype(jnp.float32).sum(0)
+    coupling_rows = lax.all_gather(coupling_col, "row", axis=0, tiled=False).sum(0)
     coupling = lax.all_to_all(
-        jnp.broadcast_to(mine[None], (n_all, span)), ("col", "row"), 0, 0, tiled=True
+        jnp.broadcast_to(coupling_rows[None], (n_col, strip, width)), "col", 0, 0, tiled=True
     ).reshape(width, width)
     trail = l21_bar - row_share - col_share
     a21_bar = jnp.dot(trail, inverse, precision=highest)

time: 201 us -> 196 us (0.975)
  blocking collectives: 25.4 us -> 51.3 us
  waiting for transfers between devices: 67 us -> 41.9 us
  starting transfers between devices: 34.4 us -> 30.8 us
  other arithmetic: 50.3 us -> 48.1 us
    all_gather x0 -> x1, blocking collectives: none -> 25.9 us  [body(): lax.all_gather(coupling_col, 'row', axis=0, tiled=False).sum(0)]
    all_to_all x2, waiting for transfers between devices: 34.8 us -> 10.5 us  [the longest x1 10.5 us: body(): lax.all_to_all(jnp.broadcast_to(coupling_rows[None], (n_col, strip, width...]
    all_to_all x2, starting transfers between devices: 14.4 us -> 10.8 us  [the longest x1 5.4 us: body(): lax.all_to_all(jnp.broadcast_to(coupling_rows[None], (n_col, strip, width...]
  transfers between devices with their start and end apart: 4 -> 4, of which waited for: 3 -> 2; matrix products, arithmetic and copies ran while one was open for 4% -> 4% of each run, Pallas kernels for 0% -> 0%
where the time goes in v7:
time: 196 us; the launch traced here: 195 us
  blocking collectives  51.3 us (26%)
  other arithmetic  48.1 us (25%)
  waiting for transfers between devices  41.9 us (21%)
  starting transfers between devices  30.8 us (16%)
  matrix products  15.9 us (8%)
  local copies, waits for them, and re-layouts  6.65 us (3%)
    all_to_all x1, waiting for transfers between devices, body(): got = lax.all_to_all(pieces, 'col', 0, 0, tiled=True)  31.4 us
    all_gather x1, blocking collectives, body(): lax.all_gather(coupling_col, 'row', axis=0, tiled=False).sum(0)  25.9 us
    all_gather x1, blocking collectives, body(): panel_cols = lax.all_gather(panel_own, 'row', axis=0, tiled=True)  25.4 us
    another operation x4, other arithmetic, invert_lower(): return lax.linalg.triangular_solve(factor, eye, left_side=True, lower=True)  21.1 us
    another operation x3, other arithmetic, factor_and_invert(): last = lax.linalg.cholesky(rest, symmetrize_input=False)  12.4 us
    another operation x3, other arithmetic, factor_and_invert(): first = lax.linalg.cholesky(square[:half, :half], symmetrize_input=False)  12.4 us
    all_to_all x1, waiting for transfers between devices, body(): lax.all_to_all(jnp.broadcast_to(coupling_rows[None], (n_col, strip, width...  10.5 us
    all_to_all x1, starting transfers between devices, gather_rows(): lax.all_to_all(spread, axis, 0, 0, tiled=True).reshape(-1, part.shape[-1])  10.5 us
  transfers between devices with their start and end apart: 4, of which 2 were waited for; matrix products, arithmetic and copies ran while one was open for 4% of the time, Pallas kernels for 0%

profile of v7, /device:TPU:1, one launch (start us, length us, event | category | flops | bytes accessed | tf_op | source)
XLA Modules:
  0.0 195.5 jit_solution(10979568283343384740)
XLA Ops:
  0.6 0.9 slice.22
  1.5 11.7 %custom-call.8 = f32[128,128]{1,0:T(8,128)S(1)} custom-call(f32[128,128]{1,0:T(8,128)S(1)} %slice.22), custom_call_target="Cholesky" | custom-call | tf_op jit(solution)/shard_map/cholesky/custom-call.1 | solution.py:33
  14.6 9.8 %custom-call.9 = f32[1,128,128]{1,2,0:T(8,128)S(1)} custom-call(f32[1,128,128]{2,1,0:T(8,128)S(1)} %get-tuple-element.8), custom_call_target="InvertDiagBlocksLowerTriangular" | custom-call | tf_op jit(solution)/shard_map/triangular_solve/custom-call.0 | solution.py:27
  24.7 1.1 fusion.29
  25.8 1.1 convolution_subtract_fusion.1
  26.9 11.7 %custom-call.10 = f32[128,128]{1,0:T(8,128)S(1)} custom-call(f32[128,128]{1,0:T(8,128)S(1)} %convolution_subtract_fusion.1), custom_call_target="Cholesky" | custom-call | tf_op jit(solution)/shard_map/cholesky/custom-call.1 | solution.py:37
  40.0 10.0 %custom-call.11 = f32[1,128,128]{1,2,0:T(8,128)S(1)} custom-call(f32[1,128,128]{2,1,0:T(8,128)S(1)} %get-tuple-element.6), custom_call_target="InvertDiagBlocksLowerTriangular" | custom-call | tf_op jit(solution)/shard_map/triangular_solve/custom-call.0 | solution.py:27
  51.2 1.1 broadcast_in_dim.7
  52.3 10.5 %all-to-all-start = ((bf16[32,64,256]{2,1,0:T(8,128)(2,1)}), bf16[32,64,256]{2,1,0:T(8,128)(2,1)S(1)}, u32[]{:S(2)}, u32[]{:S(2)}) async-start(bf16[32,64,256]{2,1,0:T(8,128)(2,1)} %broadcast_in_dim.7), calls=%async_computation | async-start | bytes 2097152 | tf_op jit(solution)/shard_map/all_to_all | solution.py:55
  62.8 25.4 %all_gather.7 = bf16[1024,256]{1,0:T(8,128)(2,1)S(1)} all-gather(bf16[64,256]{1,0:T(8,128)(2,1)S(1)} %bitcast.66), channel_id=1, replica_groups=mesh['row'=16,'col'=32] {'row'}, dimensions={0}, use_global_device_ids=true | all-gather | bytes 557056 | tf_op jit(solution)/shard_map/all_gather | solution.py:75
  88.2 4.5 %fusion = bf16[2048,256]{0,1:T(8,128)(2,1)} fusion(bf16[1024,256]{1,0:T(8,128)(2,1)S(1)} %all_gather.7, bf16[2048,1024]{1,0:T(8,128)(2,1)} %bitcast.68), kind=kOutput, calls=%fused_computation.1 | convolution fusion | flops 1074266112 | bytes 5767168 | tf_op jit(solution)/shard_map/dot_general | solution.py:76
  92.7 1.5 copy.23
  94.2 1.0 copy-done.1
  95.2 3.8 %fusion.39 = f32[256,1024]{1,0:T(8,128)S(1)} fusion(bf16[2048,256]{1,0:T(8,128)(2,1)} %bitcast.64, bf16[2048,1024]{1,0:T(8,128)(2,1)} %bitcast.69), kind=kOutput, calls=%fused_computation.68 | convolution fusion | flops 1073741824 | bytes 6291456 | tf_op jit(solution)/shard_map/dot_general | solution.py:47
  99.0 0.8 fusion.40
  100.3 1.2 pad_maximum_fusion
  101.4 9.5 %all-to-all-start.1 = ((bf16[32,80,256]{2,1,0:T(8,128)(2,1)}), bf16[32,80,256]{2,1,0:T(8,128)(2,1)S(1)}, u32[]{:S(2)}, u32[]{:S(2)}) async-start(bf16[32,80,256]{2,1,0:T(8,128)(2,1)} %pad_maximum_fusion), calls=%async_computation.1 | async-start | bytes 2621440 | tf_op jit(solution)/shard_map/all_to_all | solution.py:91
  111.0 1.0 copy.25
  112.1 31.4 %all-to-all-done.1 = bf16[32,80,256]{2,1,0:T(8,128)(2,1)S(1)} async-done(((bf16[32,80,256]{2,1,0:T(8,128)(2,1)}), bf16[32,80,256]{2,1,0:T(8,128)(2,1)S(1)}, u32[]{:S(2)}, u32[]{:S(2)}) %all-to-all-start.1) | async-done | bytes 1310752 | tf_op jit(solution)/shard_map/all_to_all | solution.py:91
  143.4 5.4 %all-to-all-start.2 = ((bf16[16,64,256]{2,1,0:T(8,128)(2,1)}), bf16[16,64,256]{2,1,0:T(8,128)(2,1)S(1)}, u32[]{:S(2)}, u32[]{:S(2)}) async-start(bf16[16,64,256]{2,1,0:T(8,128)(2,1)} %bitcast.14), calls=%async_computation.2 | async-start | bytes 1048576 | tf_op jit(solution)/shard_map/all_to_all | solution.py:97
  149.0 25.9 %all-gather = f32[128,256]{1,0:T(8,128)S(1)} all-gather(f32[8,256]{1,0:T(8,128)S(1)} %add.24), channel_id=2, replica_groups=mesh['row'=16,'col'=32] {'row'}, dimensions={0}, use_global_device_ids=true | all-gather | bytes 139264 | tf_op jit(solution)/shard_map/all_gather | solution.py:101
  175.6 5.4 %all-to-all-start.3 = ((f32[32,8,256]{2,1,0:T(8,128)}), f32[32,8,256]{2,1,0:T(8,128)S(1)}, u32[]{:S(2)}, u32[]{:S(2)}) async-start(f32[32,8,256]{2,1,0:T(8,128)} %broadcast_in_dim.8), calls=%async_computation.3 | async-start | bytes 524288 | tf_op jit(solution)/shard_map/all_to_all | solution.py:102
  181.3 0.9 fusion.26
  182.2 10.5 %all-to-all-done.3 = f32[32,8,256]{2,1,0:T(8,128)S(1)} async-done(((f32[32,8,256]{2,1,0:T(8,128)}), f32[32,8,256]{2,1,0:T(8,128)S(1)}, u32[]{:S(2)}, u32[]{:S(2)}) %all-to-all-start.3) | async-done | bytes 262176 | tf_op jit(solution)/shard_map/all_to_all | solution.py:102
  (37 shorter events, 8.6 us)
Async XLA Ops:
  0.6 50.2 %copy-start = (f32[64,256]{1,0:T(8,128)S(1)}, f32[64,256]{1,0:T(8,128)}, u32[]{:S(2)}) copy-start(f32[64,256]{1,0:T(8,128)} %param.10) | copy-start | bytes 196612
  52.3 41.9 %all-to-all-start = ((bf16[32,64,256]{2,1,0:T(8,128)(2,1)}), bf16[32,64,256]{2,1,0:T(8,128)(2,1)S(1)}, u32[]{:S(2)}, u32[]{:S(2)}) async-start(bf16[32,64,256]{2,1,0:T(8,128)(2,1)} %broadcast_in_dim.7), calls=%async_computation | async-start | bytes 2097152 | tf_op jit(solution)/shard_map/all_to_all | solution.py:55
  94.2 1.0 copy-start.1
  95.2 4.7 %copy-start.3 = (f32[64,256]{1,0:T(8,128)S(1)}, f32[64,256]{1,0:T(8,128)}, u32[]{:S(2)}) copy-start(f32[64,256]{1,0:T(8,128)} %param.11) | copy-start | bytes 196612
  101.4 42.0 %all-to-all-start.1 = ((bf16[32,80,256]{2,1,0:T(8,128)(2,1)}), bf16[32,80,256]{2,1,0:T(8,128)(2,1)S(1)}, u32[]{:S(2)}, u32[]{:S(2)}) async-start(bf16[32,80,256]{2,1,0:T(8,128)(2,1)} %pad_maximum_fusion), calls=%async_computation.1 | async-start | bytes 2621440 | tf_op jit(solution)/shard_map/all_to_all | solution.py:91
  112.1 80.6 %copy-start.2 = (f32[256,256]{1,0:T(8,128)S(1)}, f32[256,256]{1,0:T(8,128)}, u32[]{:S(2)}) copy-start(f32[256,256]{1,0:T(8,128)} %param.9) | copy-start | bytes 786436
  143.4 31.5 %all-to-all-start.2 = ((bf16[16,64,256]{2,1,0:T(8,128)(2,1)}), bf16[16,64,256]{2,1,0:T(8,128)(2,1)S(1)}, u32[]{:S(2)}, u32[]{:S(2)}) async-start(bf16[16,64,256]{2,1,0:T(8,128)(2,1)} %bitcast.14), calls=%async_computation.2 | async-start | bytes 1048576 | tf_op jit(solution)/shard_map/all_to_all | solution.py:97
  175.6 17.0 %all-to-all-start.3 = ((f32[32,8,256]{2,1,0:T(8,128)}), f32[32,8,256]{2,1,0:T(8,128)S(1)}, u32[]{:S(2)}, u32[]{:S(2)}) async-start(f32[32,8,256]{2,1,0:T(8,128)} %broadcast_in_dim.8), calls=%async_computation.3 | async-start | bytes 524288 | tf_op jit(solution)/shard_map/all_to_all | solution.py:102

commit v8 on v7

--- a/solution.py
+++ b/solution.py
@@ -55,10 +55,12 @@
     return lax.all_to_all(spread, axis, 0, 0, tiled=True).reshape(-1, part.shape[-1])
 
 
-def split_pair(values):
+def split_three(values):
     high = values.astype(jnp.bfloat16)
-    low = (values - high.astype(jnp.float32)).astype(jnp.bfloat16)
-    return high, low
+    rest = values - high.astype(jnp.float32)
+    middle = rest.astype(jnp.bfloat16)
+    low = (rest - middle.astype(jnp.float32)).astype(jnp.bfloat16)
+    return high, middle, low
 
 
 def body(a11, l11_bar, a21, l21_bar, s_bar):
@@ -78,21 +80,18 @@
     panel_exact = panel_own.astype(jnp.float32)
     cross = inner_rows(panel_cols.astype(jnp.float32), backward, highest)
     coupling_part = inner_rows(l21_bar, panel_exact, highest) - cross - cross.T
-    high, low = split_pair(coupling_part)
+    parts = split_three(coupling_part)
     strip = width // n_col
     pieces = jnp.concatenate(
-        [
-            forward.astype(jnp.bfloat16).reshape(n_col, rows_own, width),
-            high.reshape(n_col, strip, width),
-            low.reshape(n_col, strip, width),
-        ],
+        [forward.astype(jnp.bfloat16).reshape(n_col, rows_own, width)]
+        + [part.reshape(n_col, strip, width) for part in parts],
         axis=1,
     )
     got = lax.all_to_all(pieces, "col", 0, 0, tiled=True)
     row_share = got[:, :rows_own].astype(jnp.float32).sum(0)
-    coupling_col = (
-        got[:, rows_own:rows_own + strip].astype(jnp.float32).sum(0)
-        + got[:, rows_own + strip:].astype(jnp.float32).sum(0)
+    coupling_col = sum(
+        got[:, rows_own + k * strip:rows_own + (k + 1) * strip].astype(jnp.float32).sum(0)
+        for k in range(len(parts))
     )
     got = lax.all_to_all(
         backward.astype(jnp.bfloat16).reshape(n_row, rows_own, width), "row", 0, 0, tiled=True

time: 196 us -> 200 us (1.020)
  waiting for transfers between devices: 41.9 us -> 44.5 us
    all_to_all x1, waiting for transfers between devices: 31.4 us -> 34 us  [body(): got = lax.all_to_all(pieces, 'col', 0, 0, tiled=True)]
where the time goes in v8:
time: 200 us; the launch traced here: 199 us
  blocking collectives  51.3 us (26%)
  other arithmetic  48.2 us (24%)
  waiting for transfers between devices  44.5 us (22%)
  starting transfers between devices  31 us (16%)
  matrix products  16.7 us (8%)
  local copies, waits for them, and re-layouts  6.63 us (3%)
    all_to_all x1, waiting for transfers between devices, body(): got = lax.all_to_all(pieces, 'col', 0, 0, tiled=True)  34 us
    all_gather x1, blocking collectives, body(): lax.all_gather(coupling_col, 'row', axis=0, tiled=False).sum(0)  25.9 us
    all_gather x1, blocking collectives, body(): panel_cols = lax.all_gather(panel_own, 'row', axis=0, tiled=True)  25.4 us
    another operation x4, other arithmetic, invert_lower(): return lax.linalg.triangular_solve(factor, eye, left_side=True, lower=True)  21.1 us
    another operation x3, other arithmetic, factor_and_invert(): last = lax.linalg.cholesky(rest, symmetrize_input=False)  12.4 us
    another operation x3, other arithmetic, factor_and_invert(): first = lax.linalg.cholesky(square[:half, :half], symmetrize_input=False)  12.4 us
    all_to_all x1, waiting for transfers between devices, body(): lax.all_to_all(jnp.broadcast_to(coupling_rows[None], (n_col, strip, width...  10.5 us
    all_to_all x1, starting transfers between devices, gather_rows(): lax.all_to_all(spread, axis, 0, 0, tiled=True).reshape(-1, part.shape[-1])  10.5 us
  transfers between devices with their start and end apart: 4, of which 2 were waited for; matrix products, arithmetic and copies ran while one was open for 4% of the time, Pallas kernels for 0%

profile of v8, /device:TPU:1, one launch (start us, length us, event | category | flops | bytes accessed | tf_op | source)
XLA Modules:
  0.0 199.1 jit_solution(17292925130940130358)
XLA Ops:
  0.6 0.9 slice.25
  1.5 11.7 %custom-call.8 = f32[128,128]{1,0:T(8,128)S(1)} custom-call(f32[128,128]{1,0:T(8,128)S(1)} %slice.25), custom_call_target="Cholesky" | custom-call | tf_op jit(solution)/shard_map/cholesky/custom-call.1 | solution.py:33
  14.6 9.8 %custom-call.9 = f32[1,128,128]{1,2,0:T(8,128)S(1)} custom-call(f32[1,128,128]{2,1,0:T(8,128)S(1)} %get-tuple-element.9), custom_call_target="InvertDiagBlocksLowerTriangular" | custom-call | tf_op jit(solution)/shard_map/triangular_solve/custom-call.0 | solution.py:27
  24.7 1.1 fusion.31
  25.8 1.1 convolution_subtract_fusion.1
  26.9 11.7 %custom-call.10 = f32[128,128]{1,0:T(8,128)S(1)} custom-call(f32[128,128]{1,0:T(8,128)S(1)} %convolution_subtract_fusion.1), custom_call_target="Cholesky" | custom-call | tf_op jit(solution)/shard_map/cholesky/custom-call.1 | solution.py:37
  40.0 10.0 %custom-call.11 = f32[1,128,128]{1,2,0:T(8,128)S(1)} custom-call(f32[1,128,128]{2,1,0:T(8,128)S(1)} %get-tuple-element.7), custom_call_target="InvertDiagBlocksLowerTriangular" | custom-call | tf_op jit(solution)/shard_map/triangular_solve/custom-call.0 | solution.py:27
  51.2 1.1 broadcast_in_dim.7
  52.3 10.5 %all-to-all-start = ((bf16[32,64,256]{2,1,0:T(8,128)(2,1)}), bf16[32,64,256]{2,1,0:T(8,128)(2,1)S(1)}, u32[]{:S(2)}, u32[]{:S(2)}) async-start(bf16[32,64,256]{2,1,0:T(8,128)(2,1)} %broadcast_in_dim.7), calls=%async_computation | async-start | bytes 2097152 | tf_op jit(solution)/shard_map/all_to_all | solution.py:55
  62.8 25.4 %all_gather.7 = bf16[1024,256]{1,0:T(8,128)(2,1)S(1)} all-gather(bf16[64,256]{1,0:T(8,128)(2,1)S(1)} %bitcast.68), channel_id=1, replica_groups=mesh['row'=16,'col'=32] {'row'}, dimensions={0}, use_global_device_ids=true | all-gather | bytes 557056 | tf_op jit(solution)/shard_map/all_gather | solution.py:77
  88.2 4.5 %fusion = bf16[2048,256]{0,1:T(8,128)(2,1)} fusion(bf16[1024,256]{1,0:T(8,128)(2,1)S(1)} %all_gather.7, bf16[2048,1024]{1,0:T(8,128)(2,1)} %bitcast.70), kind=kOutput, calls=%fused_computation.1 | convolution fusion | flops 1074266112 | bytes 5767168 | tf_op jit(solution)/shard_map/dot_general | solution.py:78
  92.7 1.5 copy.24
  94.2 1.0 copy-done.1
  95.2 3.8 %fusion.41 = f32[256,1024]{1,0:T(8,128)S(1)} fusion(bf16[2048,256]{1,0:T(8,128)(2,1)} %bitcast.66, bf16[2048,1024]{1,0:T(8,128)(2,1)} %bitcast.71), kind=kOutput, calls=%fused_computation.73 | convolution fusion | flops 1073741824 | bytes 6291456 | tf_op jit(solution)/shard_map/dot_general | solution.py:47
  99.9 1.2 convert_bitcast_fusion.1
  101.1 1.2 pad_maximum_fusion
  102.3 9.5 %all-to-all-start.1 = ((bf16[32,88,256]{2,1,0:T(8,128)(2,1)}), bf16[32,88,256]{2,1,0:T(8,128)(2,1)S(1)}, u32[]{:S(2)}, u32[]{:S(2)}) async-start(bf16[32,88,256]{2,1,0:T(8,128)(2,1)} %pad_maximum_fusion), calls=%async_computation.1 | async-start | bytes 2883584 | tf_op jit(solution)/shard_map/all_to_all | solution.py:90
  111.9 1.0 copy.26
  112.9 34.0 %all-to-all-done.1 = bf16[32,88,256]{2,1,0:T(8,128)(2,1)S(1)} async-done(((bf16[32,88,256]{2,1,0:T(8,128)(2,1)}), bf16[32,88,256]{2,1,0:T(8,128)(2,1)S(1)}, u32[]{:S(2)}, u32[]{:S(2)}) %all-to-all-start.1) | async-done | bytes 1441824 | tf_op jit(solution)/shard_map/all_to_all | solution.py:90
  146.9 5.6 %all-to-all-start.2 = ((bf16[16,64,256]{2,1,0:T(8,128)(2,1)}), bf16[16,64,256]{2,1,0:T(8,128)(2,1)S(1)}, u32[]{:S(2)}, u32[]{:S(2)}) async-start(bf16[16,64,256]{2,1,0:T(8,128)(2,1)} %bitcast.15), calls=%async_computation.2 | async-start | bytes 1048576 | tf_op jit(solution)/shard_map/all_to_all | solution.py:96
  152.7 25.9 %all-gather = f32[128,256]{1,0:T(8,128)S(1)} all-gather(f32[8,256]{1,0:T(8,128)S(1)} %add_add_fusion), channel_id=2, replica_groups=mesh['row'=16,'col'=32] {'row'}, dimensions={0}, use_global_device_ids=true | all-gather | bytes 139264 | tf_op jit(solution)/shard_map/all_gather | solution.py:100
  179.3 5.4 %all-to-all-start.3 = ((f32[32,8,256]{2,1,0:T(8,128)}), f32[32,8,256]{2,1,0:T(8,128)S(1)}, u32[]{:S(2)}, u32[]{:S(2)}) async-start(f32[32,8,256]{2,1,0:T(8,128)} %broadcast_in_dim.8), calls=%async_computation.3 | async-start | bytes 524288 | tf_op jit(solution)/shard_map/all_to_all | solution.py:101
  185.0 0.9 fusion.28
  185.9 10.5 %all-to-all-done.3 = f32[32,8,256]{2,1,0:T(8,128)S(1)} async-done(((f32[32,8,256]{2,1,0:T(8,128)}), f32[32,8,256]{2,1,0:T(8,128)S(1)}, u32[]{:S(2)}, u32[]{:S(2)}) %all-to-all-start.3) | async-done | bytes 262176 | tf_op jit(solution)/shard_map/all_to_all | solution.py:101
  (37 shorter events, 9.0 us)
Async XLA Ops:
  0.6 50.2 %copy-start = (f32[64,256]{1,0:T(8,128)S(1)}, f32[64,256]{1,0:T(8,128)}, u32[]{:S(2)}) copy-start(f32[64,256]{1,0:T(8,128)} %param.10) | copy-start | bytes 196612
  52.3 41.9 %all-to-all-start = ((bf16[32,64,256]{2,1,0:T(8,128)(2,1)}), bf16[32,64,256]{2,1,0:T(8,128)(2,1)S(1)}, u32[]{:S(2)}, u32[]{:S(2)}) async-start(bf16[32,64,256]{2,1,0:T(8,128)(2,1)} %broadcast_in_dim.7), calls=%async_computation | async-start | bytes 2097152 | tf_op jit(solution)/shard_map/all_to_all | solution.py:55
  94.2 1.0 copy-start.1
  102.3 44.6 %all-to-all-start.1 = ((bf16[32,88,256]{2,1,0:T(8,128)(2,1)}), bf16[32,88,256]{2,1,0:T(8,128)(2,1)S(1)}, u32[]{:S(2)}, u32[]{:S(2)}) async-start(bf16[32,88,256]{2,1,0:T(8,128)(2,1)} %pad_maximum_fusion), calls=%async_computation.1 | async-start | bytes 2883584 | tf_op jit(solution)/shard_map/all_to_all | solution.py:90
  111.9 84.5 %copy-start.2 = (f32[256,256]{1,0:T(8,128)S(1)}, f32[256,256]{1,0:T(8,128)}, u32[]{:S(2)}) copy-start(f32[256,256]{1,0:T(8,128)} %param.9) | copy-start | bytes 786436
  112.9 72.0 %copy-start.3 = (f32[64,256]{1,0:T(8,128)S(1)}, f32[64,256]{1,0:T(8,128)}, u32[]{:S(2)}) copy-start(f32[64,256]{1,0:T(8,128)} %param.11) | copy-start | bytes 196612
  146.9 31.6 %all-to-all-start.2 = ((bf16[16,64,256]{2,1,0:T(8,128)(2,1)}), bf16[16,64,256]{2,1,0:T(8,128)(2,1)S(1)}, u32[]{:S(2)}, u32[]{:S(2)}) async-start(bf16[16,64,256]{2,1,0:T(8,128)(2,1)} %bitcast.15), calls=%async_computation.2 | async-start | bytes 1048576 | tf_op jit(solution)/shard_map/all_to_all | solution.py:96
  179.3 17.1 %all-to-all-start.3 = ((f32[32,8,256]{2,1,0:T(8,128)}), f32[32,8,256]{2,1,0:T(8,128)S(1)}, u32[]{:S(2)}, u32[]{:S(2)}) async-start(f32[32,8,256]{2,1,0:T(8,128)} %broadcast_in_dim.8), calls=%async_computation.3 | async-start | bytes 524288 | tf_op jit(solution)/shard_map/all_to_all | solution.py:101

commit v9 on v7

--- a/solution.py
+++ b/solution.py
@@ -56,9 +56,9 @@
 
 
 def split_pair(values):
-    high = values.astype(jnp.bfloat16)
-    low = (values - high.astype(jnp.float32)).astype(jnp.bfloat16)
-    return high, low
+    high = lax.reduce_precision(values, exponent_bits=8, mantissa_bits=7)
+    low = values - high
+    return high.astype(jnp.bfloat16), low.astype(jnp.bfloat16)
 
 
 def body(a11, l11_bar, a21, l21_bar, s_bar):

time: 196 us -> 196 us (level)
  no operation moved by 1% of the time
where the time goes in v9:
time: 196 us; the launch traced here: 195 us
  blocking collectives  51.3 us (26%)
  other arithmetic  48.1 us (25%)
  waiting for transfers between devices  41.9 us (21%)
  starting transfers between devices  30.8 us (16%)
  matrix products  15.9 us (8%)
  local copies, waits for them, and re-layouts  6.65 us (3%)
    all_to_all x1, waiting for transfers between devices, body(): got = lax.all_to_all(pieces, 'col', 0, 0, tiled=True)  31.4 us
    all_gather x1, blocking collectives, body(): lax.all_gather(coupling_col, 'row', axis=0, tiled=False).sum(0)  25.9 us
    all_gather x1, blocking collectives, body(): panel_cols = lax.all_gather(panel_own, 'row', axis=0, tiled=True)  25.4 us
    another operation x4, other arithmetic, invert_lower(): return lax.linalg.triangular_solve(factor, eye, left_side=True, lower=True)  21.1 us
    another operation x3, other arithmetic, factor_and_invert(): last = lax.linalg.cholesky(rest, symmetrize_input=False)  12.4 us
    another operation x3, other arithmetic, factor_and_invert(): first = lax.linalg.cholesky(square[:half, :half], symmetrize_input=False)  12.4 us
    all_to_all x1, waiting for transfers between devices, body(): lax.all_to_all(jnp.broadcast_to(coupling_rows[None], (n_col, strip, width...  10.5 us
    all_to_all x1, starting transfers between devices, gather_rows(): lax.all_to_all(spread, axis, 0, 0, tiled=True).reshape(-1, part.shape[-1])  10.5 us
  transfers between devices with their start and end apart: 4, of which 2 were waited for; matrix products, arithmetic and copies ran while one was open for 4% of the time, Pallas kernels for 0%

profile of v9, /device:TPU:1, one launch (start us, length us, event | category | flops | bytes accessed | tf_op | source)
XLA Modules:
  0.0 195.5 jit_solution(1303448231900896672)
XLA Ops:
  0.6 0.9 slice.22
  1.5 11.7 %custom-call.8 = f32[128,128]{1,0:T(8,128)S(1)} custom-call(f32[128,128]{1,0:T(8,128)S(1)} %slice.22), custom_call_target="Cholesky" | custom-call | tf_op jit(solution)/shard_map/cholesky/custom-call.1 | solution.py:33
  14.6 9.8 %custom-call.9 = f32[1,128,128]{1,2,0:T(8,128)S(1)} custom-call(f32[1,128,128]{2,1,0:T(8,128)S(1)} %get-tuple-element.8), custom_call_target="InvertDiagBlocksLowerTriangular" | custom-call | tf_op jit(solution)/shard_map/triangular_solve/custom-call.0 | solution.py:27
  24.7 1.1 fusion.31
  25.8 1.1 convolution_subtract_fusion.1
  26.9 11.7 %custom-call.10 = f32[128,128]{1,0:T(8,128)S(1)} custom-call(f32[128,128]{1,0:T(8,128)S(1)} %convolution_subtract_fusion.1), custom_call_target="Cholesky" | custom-call | tf_op jit(solution)/shard_map/cholesky/custom-call.1 | solution.py:37
  40.0 10.0 %custom-call.11 = f32[1,128,128]{1,2,0:T(8,128)S(1)} custom-call(f32[1,128,128]{2,1,0:T(8,128)S(1)} %get-tuple-element.6), custom_call_target="InvertDiagBlocksLowerTriangular" | custom-call | tf_op jit(solution)/shard_map/triangular_solve/custom-call.0 | solution.py:27
  51.2 1.1 broadcast_in_dim.7
  52.3 10.5 %all-to-all-start = ((bf16[32,64,256]{2,1,0:T(8,128)(2,1)}), bf16[32,64,256]{2,1,0:T(8,128)(2,1)S(1)}, u32[]{:S(2)}, u32[]{:S(2)}) async-start(bf16[32,64,256]{2,1,0:T(8,128)(2,1)} %broadcast_in_dim.7), calls=%async_computation | async-start | bytes 2097152 | tf_op jit(solution)/shard_map/all_to_all | solution.py:55
  62.8 25.4 %all_gather.7 = bf16[1024,256]{1,0:T(8,128)(2,1)S(1)} all-gather(bf16[64,256]{1,0:T(8,128)(2,1)S(1)} %bitcast.66), channel_id=1, replica_groups=mesh['row'=16,'col'=32] {'row'}, dimensions={0}, use_global_device_ids=true | all-gather | bytes 557056 | tf_op jit(solution)/shard_map/all_gather | solution.py:75
  88.2 4.5 %fusion = bf16[2048,256]{0,1:T(8,128)(2,1)} fusion(bf16[1024,256]{1,0:T(8,128)(2,1)S(1)} %all_gather.7, bf16[2048,1024]{1,0:T(8,128)(2,1)} %bitcast.68), kind=kOutput, calls=%fused_computation.1 | convolution fusion | flops 1074266112 | bytes 5767168 | tf_op jit(solution)/shard_map/dot_general | solution.py:76
  92.7 1.5 copy.23
  94.2 1.0 copy-done.1
  95.2 3.8 %fusion.41 = f32[256,1024]{1,0:T(8,128)S(1)} fusion(bf16[2048,256]{1,0:T(8,128)(2,1)} %bitcast.64, bf16[2048,1024]{1,0:T(8,128)(2,1)} %bitcast.69), kind=kOutput, calls=%fused_computation.70 | convolution fusion | flops 1073741824 | bytes 6291456 | tf_op jit(solution)/shard_map/dot_general | solution.py:47
  99.0 0.8 fusion.42
  100.3 1.2 pad_maximum_fusion
  101.4 9.5 %all-to-all-start.1 = ((bf16[32,80,256]{2,1,0:T(8,128)(2,1)}), bf16[32,80,256]{2,1,0:T(8,128)(2,1)S(1)}, u32[]{:S(2)}, u32[]{:S(2)}) async-start(bf16[32,80,256]{2,1,0:T(8,128)(2,1)} %pad_maximum_fusion), calls=%async_computation.1 | async-start | bytes 2621440 | tf_op jit(solution)/shard_map/all_to_all | solution.py:91
  111.0 1.0 copy.25
  112.1 31.4 %all-to-all-done.1 = bf16[32,80,256]{2,1,0:T(8,128)(2,1)S(1)} async-done(((bf16[32,80,256]{2,1,0:T(8,128)(2,1)}), bf16[32,80,256]{2,1,0:T(8,128)(2,1)S(1)}, u32[]{:S(2)}, u32[]{:S(2)}) %all-to-all-start.1) | async-done | bytes 1310752 | tf_op jit(solution)/shard_map/all_to_all | solution.py:91
  143.4 5.4 %all-to-all-start.2 = ((bf16[16,64,256]{2,1,0:T(8,128)(2,1)}), bf16[16,64,256]{2,1,0:T(8,128)(2,1)S(1)}, u32[]{:S(2)}, u32[]{:S(2)}) async-start(bf16[16,64,256]{2,1,0:T(8,128)(2,1)} %bitcast.14), calls=%async_computation.2 | async-start | bytes 1048576 | tf_op jit(solution)/shard_map/all_to_all | solution.py:97
  149.0 25.9 %all-gather = f32[128,256]{1,0:T(8,128)S(1)} all-gather(f32[8,256]{1,0:T(8,128)S(1)} %add.24), channel_id=2, replica_groups=mesh['row'=16,'col'=32] {'row'}, dimensions={0}, use_global_device_ids=true | all-gather | bytes 139264 | tf_op jit(solution)/shard_map/all_gather | solution.py:101
  175.6 5.4 %all-to-all-start.3 = ((f32[32,8,256]{2,1,0:T(8,128)}), f32[32,8,256]{2,1,0:T(8,128)S(1)}, u32[]{:S(2)}, u32[]{:S(2)}) async-start(f32[32,8,256]{2,1,0:T(8,128)} %broadcast_in_dim.8), calls=%async_computation.3 | async-start | bytes 524288 | tf_op jit(solution)/shard_map/all_to_all | solution.py:102
  181.3 0.9 fusion.28
  182.2 10.5 %all-to-all-done.3 = f32[32,8,256]{2,1,0:T(8,128)S(1)} async-done(((f32[32,8,256]{2,1,0:T(8,128)}), f32[32,8,256]{2,1,0:T(8,128)S(1)}, u32[]{:S(2)}, u32[]{:S(2)}) %all-to-all-start.3) | async-done | bytes 262176 | tf_op jit(solution)/shard_map/all_to_all | solution.py:102
  (37 shorter events, 8.6 us)
Async XLA Ops:
  0.6 50.2 %copy-start = (f32[64,256]{1,0:T(8,128)S(1)}, f32[64,256]{1,0:T(8,128)}, u32[]{:S(2)}) copy-start(f32[64,256]{1,0:T(8,128)} %param.10) | copy-start | bytes 196612
  52.3 41.9 %all-to-all-start = ((bf16[32,64,256]{2,1,0:T(8,128)(2,1)}), bf16[32,64,256]{2,1,0:T(8,128)(2,1)S(1)}, u32[]{:S(2)}, u32[]{:S(2)}) async-start(bf16[32,64,256]{2,1,0:T(8,128)(2,1)} %broadcast_in_dim.7), calls=%async_computation | async-start | bytes 2097152 | tf_op jit(solution)/shard_map/all_to_all | solution.py:55
  94.2 1.0 copy-start.1
  95.2 4.7 %copy-start.3 = (f32[64,256]{1,0:T(8,128)S(1)}, f32[64,256]{1,0:T(8,128)}, u32[]{:S(2)}) copy-start(f32[64,256]{1,0:T(8,128)} %param.11) | copy-start | bytes 196612
  101.4 42.0 %all-to-all-start.1 = ((bf16[32,80,256]{2,1,0:T(8,128)(2,1)}), bf16[32,80,256]{2,1,0:T(8,128)(2,1)S(1)}, u32[]{:S(2)}, u32[]{:S(2)}) async-start(bf16[32,80,256]{2,1,0:T(8,128)(2,1)} %pad_maximum_fusion), calls=%async_computation.1 | async-start | bytes 2621440 | tf_op jit(solution)/shard_map/all_to_all | solution.py:91
  112.1 80.6 %copy-start.2 = (f32[256,256]{1,0:T(8,128)S(1)}, f32[256,256]{1,0:T(8,128)}, u32[]{:S(2)}) copy-start(f32[256,256]{1,0:T(8,128)} %param.9) | copy-start | bytes 786436
  143.4 31.5 %all-to-all-start.2 = ((bf16[16,64,256]{2,1,0:T(8,128)(2,1)}), bf16[16,64,256]{2,1,0:T(8,128)(2,1)S(1)}, u32[]{:S(2)}, u32[]{:S(2)}) async-start(bf16[16,64,256]{2,1,0:T(8,128)(2,1)} %bitcast.14), calls=%async_computation.2 | async-start | bytes 1048576 | tf_op jit(solution)/shard_map/all_to_all | solution.py:97
  175.6 17.0 %all-to-all-start.3 = ((f32[32,8,256]{2,1,0:T(8,128)}), f32[32,8,256]{2,1,0:T(8,128)S(1)}, u32[]{:S(2)}, u32[]{:S(2)}) async-start(f32[32,8,256]{2,1,0:T(8,128)} %broadcast_in_dim.8), calls=%async_computation.3 | async-start | bytes 524288 | tf_op jit(solution)/shard_map/all_to_all | solution.py:102

commit v10 on v9

--- a/solution.py
+++ b/solution.py
@@ -1,6 +1,7 @@
 import jax
 import jax.numpy as jnp
 from jax import lax
+from jax.experimental.layout import Layout, with_layout_constraint
 from jax.sharding import PartitionSpec as P
 
 
@@ -82,7 +83,7 @@
     strip = width // n_col
     pieces = jnp.concatenate(
         [
-            forward.astype(jnp.bfloat16).reshape(n_col, rows_own, width),
+            with_layout_constraint(forward.astype(jnp.bfloat16), Layout((0, 1))).reshape(n_col, rows_own, width),
             high.reshape(n_col, strip, width),
             low.reshape(n_col, strip, width),
         ],
@@ -95,7 +96,8 @@
         + got[:, rows_own + strip:].astype(jnp.float32).sum(0)
     )
     got = lax.all_to_all(
-        backward.astype(jnp.bfloat16).reshape(n_row, rows_own, width), "row", 0, 0, tiled=True
+        with_layout_constraint(backward.astype(jnp.bfloat16), Layout((0, 1))).reshape(n_row, rows_own, width),
+        "row", 0, 0, tiled=True,
     )
     col_share = got.astype(jnp.float32).sum(0)
     coupling_rows = lax.all_gather(coupling_col, "row", axis=0, tiled=False).sum(0)

time: 196 us -> 196 us (level)
    convert_element_type x2 -> x0, local copies, waits for them, and re-layouts: 2.51 us -> none  [the longest x1 1.47 us: body(): forward.astype(jnp.bfloat16).reshape(n_col, rows_own, width)]
  transfers between devices with their start and end apart: 4 -> 4, of which waited for: 2 -> 2; matrix products, arithmetic and copies ran while one was open for 4% -> 3% of each run, Pallas kernels for 0% -> 0%
where the time goes in v10:
time: 196 us; the launch traced here: 195 us
  blocking collectives  51.1 us (26%)
  other arithmetic  49.3 us (25%)
  waiting for transfers between devices  42 us (21%)
  starting transfers between devices  31 us (16%)
  matrix products  15.8 us (8%)
  local copies, waits for them, and re-layouts  5.19 us (3%)
    all_to_all x1, waiting for transfers between devices, body(): got = lax.all_to_all(pieces, 'col', 0, 0, tiled=True)  31.5 us
    all_gather x1, blocking collectives, body(): lax.all_gather(coupling_col, 'row', axis=0, tiled=False).sum(0)  25.7 us
    all_gather x1, blocking collectives, body(): panel_cols = lax.all_gather(panel_own, 'row', axis=0, tiled=True)  25.4 us
    another operation x4, other arithmetic, invert_lower(): return lax.linalg.triangular_solve(factor, eye, left_side=True, lower=True)  21.1 us
    another operation x3, other arithmetic, factor_and_invert(): last = lax.linalg.cholesky(rest, symmetrize_input=False)  12.4 us
    another operation x3, other arithmetic, factor_and_invert(): first = lax.linalg.cholesky(square[:half, :half], symmetrize_input=False)  12.4 us
    all_to_all x1, waiting for transfers between devices, body(): lax.all_to_all(jnp.broadcast_to(coupling_rows[None], (n_col, strip, width...  10.5 us
    all_to_all x1, starting transfers between devices, gather_rows(): lax.all_to_all(spread, axis, 0, 0, tiled=True).reshape(-1, part.shape[-1])  10.5 us
  transfers between devices with their start and end apart: 4, of which 2 were waited for; matrix products, arithmetic and copies ran while one was open for 3% of the time, Pallas kernels for 0%

profile of v10, /device:TPU:1, one launch (start us, length us, event | category | flops | bytes accessed | tf_op | source)
XLA Modules:
  0.0 195.1 jit_solution(16280999817730816670)
XLA Ops:
  0.6 0.9 slice.22
  1.5 11.7 %custom-call.8 = f32[128,128]{1,0:T(8,128)S(1)} custom-call(f32[128,128]{1,0:T(8,128)S(1)} %slice.22), custom_call_target="Cholesky" | custom-call | tf_op jit(solution)/shard_map/cholesky/custom-call.1 | solution.py:34
  14.6 9.8 %custom-call.9 = f32[1,128,128]{1,2,0:T(8,128)S(1)} custom-call(f32[1,128,128]{2,1,0:T(8,128)S(1)} %get-tuple-element.8), custom_call_target="InvertDiagBlocksLowerTriangular" | custom-call | tf_op jit(solution)/shard_map/triangular_solve/custom-call.0 | solution.py:28
  24.7 1.1 fusion.30
  25.8 1.1 convolution_subtract_fusion.1
  26.9 11.7 %custom-call.10 = f32[128,128]{1,0:T(8,128)S(1)} custom-call(f32[128,128]{1,0:T(8,128)S(1)} %convolution_subtract_fusion.1), custom_call_target="Cholesky" | custom-call | tf_op jit(solution)/shard_map/cholesky/custom-call.1 | solution.py:38
  40.0 10.0 %custom-call.11 = f32[1,128,128]{1,2,0:T(8,128)S(1)} custom-call(f32[1,128,128]{2,1,0:T(8,128)S(1)} %get-tuple-element.6), custom_call_target="InvertDiagBlocksLowerTriangular" | custom-call | tf_op jit(solution)/shard_map/triangular_solve/custom-call.0 | solution.py:28
  51.2 1.1 broadcast_in_dim.7
  52.3 10.5 %all-to-all-start = ((bf16[32,64,256]{2,1,0:T(8,128)(2,1)}), bf16[32,64,256]{2,1,0:T(8,128)(2,1)S(1)}, u32[]{:S(2)}, u32[]{:S(2)}) async-start(bf16[32,64,256]{2,1,0:T(8,128)(2,1)} %broadcast_in_dim.7), calls=%async_computation | async-start | bytes 2097152 | tf_op jit(solution)/shard_map/all_to_all | solution.py:56
  62.8 25.4 %all_gather.7 = bf16[1024,256]{1,0:T(8,128)(2,1)S(1)} all-gather(bf16[64,256]{1,0:T(8,128)(2,1)S(1)} %bitcast.66), channel_id=1, replica_groups=mesh['row'=16,'col'=32] {'row'}, dimensions={0}, use_global_device_ids=true | all-gather | bytes 557056 | tf_op jit(solution)/shard_map/all_gather | solution.py:76
  88.2 4.4 %convolution_convert_fusion = bf16[256,2048]{0,1:T(8,128)(2,1)} fusion(bf16[2048,1024]{1,0:T(8,128)(2,1)} %bitcast.68, bf16[1024,256]{1,0:T(8,128)(2,1)S(1)} %all_gather.7), kind=kOutput, calls=%fused_computation | convolution fusion | flops 1074266112 | bytes 5767168 | tf_op jit(solution)/shard_map/dot_general | solution.py:77
  92.6 1.0 copy-done.1
  93.6 3.8 %fusion.40 = f32[256,1024]{1,0:T(8,128)S(1)} fusion(bf16[2048,256]{1,0:T(8,128)(2,1)} %bitcast.64, bf16[2048,1024]{1,0:T(8,128)(2,1)} %bitcast.69), kind=kOutput, calls=%fused_computation.68 | convolution fusion | flops 1073741824 | bytes 6291456 | tf_op jit(solution)/shard_map/dot_general | solution.py:48
  97.4 0.8 fusion.41
  98.7 2.4 %pad_maximum_fusion = bf16[32,80,256]{2,1,0:T(8,128)(2,1)} fusion(bf16[32,8,256]{2,1,0:T(8,128)(2,1)S(1)} %get-tuple-element.11, bf16[32,8,256]{2,1,0:T(8,128)(2,1)S(1)} %get-tuple-element.10, bf16[32,64,256]{2,1,0:T(8,128)(2,1)} %bitcast.63), kind=kLoop, calls=%fused_computation.2 | loop fusion | flops 3932160 | bytes 2621440 | tf_op jit(solution)/shard_map/concatenate | solution.py:84
  101.1 9.5 %all-to-all-start.1 = ((bf16[32,80,256]{2,1,0:T(8,128)(2,1)}), bf16[32,80,256]{2,1,0:T(8,128)(2,1)S(1)}, u32[]{:S(2)}, u32[]{:S(2)}) async-start(bf16[32,80,256]{2,1,0:T(8,128)(2,1)} %pad_maximum_fusion), calls=%async_computation.1 | async-start | bytes 2621440 | tf_op jit(solution)/shard_map/all_to_all | solution.py:92
  110.6 1.0 copy.16
  111.6 31.5 %all-to-all-done.1 = bf16[32,80,256]{2,1,0:T(8,128)(2,1)S(1)} async-done(((bf16[32,80,256]{2,1,0:T(8,128)(2,1)}), bf16[32,80,256]{2,1,0:T(8,128)(2,1)S(1)}, u32[]{:S(2)}, u32[]{:S(2)}) %all-to-all-start.1) | async-done | bytes 1310752 | tf_op jit(solution)/shard_map/all_to_all | solution.py:92
  143.1 5.6 %all-to-all-start.2 = ((bf16[16,64,256]{2,1,0:T(8,128)(2,1)}), bf16[16,64,256]{2,1,0:T(8,128)(2,1)S(1)}, u32[]{:S(2)}, u32[]{:S(2)}) async-start(bf16[16,64,256]{2,1,0:T(8,128)(2,1)} %bitcast.14), calls=%async_computation.2 | async-start | bytes 1048576 | tf_op jit(solution)/shard_map/all_to_all | solution.py:98
  148.9 25.7 %all-gather = f32[128,256]{1,0:T(8,128)S(1)} all-gather(f32[8,256]{1,0:T(8,128)S(1)} %add.24), channel_id=2, replica_groups=mesh['row'=16,'col'=32] {'row'}, dimensions={0}, use_global_device_ids=true | all-gather | bytes 139264 | tf_op jit(solution)/shard_map/all_gather | solution.py:103
  175.3 5.4 %all-to-all-start.3 = ((f32[32,8,256]{2,1,0:T(8,128)}), f32[32,8,256]{2,1,0:T(8,128)S(1)}, u32[]{:S(2)}, u32[]{:S(2)}) async-start(f32[32,8,256]{2,1,0:T(8,128)} %broadcast_in_dim.8), calls=%async_computation.3 | async-start | bytes 524288 | tf_op jit(solution)/shard_map/all_to_all | solution.py:104
  180.9 0.9 fusion.27
  181.8 10.5 %all-to-all-done.3 = f32[32,8,256]{2,1,0:T(8,128)S(1)} async-done(((f32[32,8,256]{2,1,0:T(8,128)}), f32[32,8,256]{2,1,0:T(8,128)S(1)}, u32[]{:S(2)}, u32[]{:S(2)}) %all-to-all-start.3) | async-done | bytes 262176 | tf_op jit(solution)/shard_map/all_to_all | solution.py:104
  194.4 0.7 fusion.8
  (35 shorter events, 7.8 us)
Async XLA Ops:
  0.6 50.2 %copy-start = (f32[64,256]{1,0:T(8,128)S(1)}, f32[64,256]{1,0:T(8,128)}, u32[]{:S(2)}) copy-start(f32[64,256]{1,0:T(8,128)} %param.10) | copy-start | bytes 196612
  52.3 40.3 %all-to-all-start = ((bf16[32,64,256]{2,1,0:T(8,128)(2,1)}), bf16[32,64,256]{2,1,0:T(8,128)(2,1)S(1)}, u32[]{:S(2)}, u32[]{:S(2)}) async-start(bf16[32,64,256]{2,1,0:T(8,128)(2,1)} %broadcast_in_dim.7), calls=%async_computation | async-start | bytes 2097152 | tf_op jit(solution)/shard_map/all_to_all | solution.py:56
  92.6 1.0 copy-start.1
  93.6 4.7 %copy-start.3 = (f32[64,256]{1,0:T(8,128)S(1)}, f32[64,256]{1,0:T(8,128)}, u32[]{:S(2)}) copy-start(f32[64,256]{1,0:T(8,128)} %param.11) | copy-start | bytes 196612
  101.1 42.0 %all-to-all-start.1 = ((bf16[32,80,256]{2,1,0:T(8,128)(2,1)}), bf16[32,80,256]{2,1,0:T(8,128)(2,1)S(1)}, u32[]{:S(2)}, u32[]{:S(2)}) async-start(bf16[32,80,256]{2,1,0:T(8,128)(2,1)} %pad_maximum_fusion), calls=%async_computation.1 | async-start | bytes 2621440 | tf_op jit(solution)/shard_map/all_to_all | solution.py:92
  111.6 80.7 %copy-start.2 = (f32[256,256]{1,0:T(8,128)S(1)}, f32[256,256]{1,0:T(8,128)}, u32[]{:S(2)}) copy-start(f32[256,256]{1,0:T(8,128)} %param.9) | copy-start | bytes 786436
  143.1 31.5 %all-to-all-start.2 = ((bf16[16,64,256]{2,1,0:T(8,128)(2,1)}), bf16[16,64,256]{2,1,0:T(8,128)(2,1)S(1)}, u32[]{:S(2)}, u32[]{:S(2)}) async-start(bf16[16,64,256]{2,1,0:T(8,128)(2,1)} %bitcast.14), calls=%async_computation.2 | async-start | bytes 1048576 | tf_op jit(solution)/shard_map/all_to_all | solution.py:98
  175.3 17.0 %all-to-all-start.3 = ((f32[32,8,256]{2,1,0:T(8,128)}), f32[32,8,256]{2,1,0:T(8,128)S(1)}, u32[]{:S(2)}, u32[]{:S(2)}) async-start(f32[32,8,256]{2,1,0:T(8,128)} %broadcast_in_dim.8), calls=%async_computation.3 | async-start | bytes 524288 | tf_op jit(solution)/shard_map/all_to_all | solution.py:104

commit v11 on v10

--- a/solution.py
+++ b/solution.py
@@ -75,7 +75,7 @@
     panel_rows = gather_rows(panel_own, "col", n_col)
     panel_cols = lax.all_gather(panel_own, "row", axis=0, tiled=True)
     forward = jnp.dot(tile, panel_cols, preferred_element_type=jnp.float32)
-    backward = inner_rows(tile, panel_rows)
+    backward = with_layout_constraint(inner_rows(tile, panel_rows), Layout((0, 1)))
     panel_exact = panel_own.astype(jnp.float32)
     cross = inner_rows(panel_cols.astype(jnp.float32), backward, highest)
     coupling_part = inner_rows(l21_bar, panel_exact, highest) - cross - cross.T

time: 196 us -> 194 us (0.990)
  blocking collectives: 51.1 us -> 95.2 us
  waiting for transfers between devices: 42 us -> 10.8 us
  starting transfers between devices: 31 us -> 20.4 us
  other arithmetic: 49.3 us -> 47 us
  local copies, waits for them, and re-layouts: 5.19 us -> 3.16 us
    all_to_all x0 -> x1, blocking collectives: none -> 44.1 us  [body(): got = lax.all_to_all(pieces, 'col', 0, 0, tiled=True)]
    all_to_all x1 -> x0, waiting for transfers between devices: 31.5 us -> none  [body(): got = lax.all_to_all(pieces, 'col', 0, 0, tiled=True)]
    all_to_all x1 -> x0, starting transfers between devices: 9.49 us -> none  [body(): got = lax.all_to_all(pieces, 'col', 0, 0, tiled=True)]
    concatenate x1, other arithmetic: 2.39 us -> 0.09 us  [body(): jnp.concatenate([with_layout_constraint(forward.astype(jnp.bfloat16), Lay...]
  transfers between devices with their start and end apart: 4 -> 3, of which waited for: 2 -> 1; matrix products, arithmetic and copies ran while one was open for 3% -> 2% of each run, Pallas kernels for 0% -> 0%
where the time goes in v11:
time: 194 us; the launch traced here: 193 us
  blocking collectives  95.2 us (49%)
  other arithmetic  47 us (24%)
  starting transfers between devices  20.4 us (11%)
  matrix products  15.7 us (8%)
  waiting for transfers between devices  10.8 us (6%)
  local copies, waits for them, and re-layouts  3.16 us (2%)
    all_to_all x1, blocking collectives, body(): got = lax.all_to_all(pieces, 'col', 0, 0, tiled=True)  44.1 us
    all_gather x1, blocking collectives, body(): lax.all_gather(coupling_col, 'row', axis=0, tiled=False).sum(0)  25.7 us
    all_gather x1, blocking collectives, body(): panel_cols = lax.all_gather(panel_own, 'row', axis=0, tiled=True)  25.4 us
    another operation x4, other arithmetic, invert_lower(): return lax.linalg.triangular_solve(factor, eye, left_side=True, lower=True)  21.1 us
    another operation x3, other arithmetic, factor_and_invert(): last = lax.linalg.cholesky(rest, symmetrize_input=False)  12.4 us
    another operation x3, other arithmetic, factor_and_invert(): first = lax.linalg.cholesky(square[:half, :half], symmetrize_input=False)  12.4 us
    all_to_all x1, waiting for transfers between devices, body(): lax.all_to_all(jnp.broadcast_to(coupling_rows[None], (n_col, strip, width...  10.8 us
    all_to_all x1, starting transfers between devices, gather_rows(): lax.all_to_all(spread, axis, 0, 0, tiled=True).reshape(-1, part.shape[-1])  10.5 us
  transfers between devices with their start and end apart: 3, of which 1 were waited for; matrix products, arithmetic and copies ran while one was open for 2% of the time, Pallas kernels for 0%

profile of v11, /device:TPU:1, one launch (start us, length us, event | category | flops | bytes accessed | tf_op | source)
XLA Modules:
  0.0 193.1 jit_solution(2921699986909413413)
XLA Ops:
  0.6 0.9 slice.22
  1.5 11.7 %custom-call.8 = f32[128,128]{1,0:T(8,128)S(1)} custom-call(f32[128,128]{1,0:T(8,128)S(1)} %slice.22), custom_call_target="Cholesky" | custom-call | tf_op jit(solution)/shard_map/cholesky/custom-call.1 | solution.py:34
  13.9 0.7 select_bitcast_fusion.1
  14.6 9.8 %custom-call.9 = f32[1,128,128]{1,2,0:T(8,128)S(1)} custom-call(f32[1,128,128]{2,1,0:T(8,128)S(1)} %get-tuple-element.8), custom_call_target="InvertDiagBlocksLowerTriangular" | custom-call | tf_op jit(solution)/shard_map/triangular_solve/custom-call.0 | solution.py:28
  24.7 1.1 fusion.30
  25.8 1.1 convolution_subtract_fusion.1
  26.9 11.7 %custom-call.10 = f32[128,128]{1,0:T(8,128)S(1)} custom-call(f32[128,128]{1,0:T(8,128)S(1)} %convolution_subtract_fusion.1), custom_call_target="Cholesky" | custom-call | tf_op jit(solution)/shard_map/cholesky/custom-call.1 | solution.py:38
  38.7 0.6 compare_reduce_fusion
  39.3 0.7 select_bitcast_fusion
  40.0 10.0 %custom-call.11 = f32[1,128,128]{1,2,0:T(8,128)S(1)} custom-call(f32[1,128,128]{2,1,0:T(8,128)S(1)} %get-tuple-element.6), custom_call_target="InvertDiagBlocksLowerTriangular" | custom-call | tf_op jit(solution)/shard_map/triangular_solve/custom-call.0 | solution.py:28
  51.2 1.1 broadcast_in_dim.7
  52.3 10.5 %all-to-all-start = ((bf16[32,64,256]{2,1,0:T(8,128)(2,1)}), bf16[32,64,256]{2,1,0:T(8,128)(2,1)S(1)}, u32[]{:S(2)}, u32[]{:S(2)}) async-start(bf16[32,64,256]{2,1,0:T(8,128)(2,1)} %broadcast_in_dim.7), calls=%async_computation | async-start | bytes 2097152 | tf_op jit(solution)/shard_map/all_to_all | solution.py:56
  62.8 25.4 %all_gather.7 = bf16[1024,256]{1,0:T(8,128)(2,1)S(1)} all-gather(bf16[64,256]{1,0:T(8,128)(2,1)S(1)} %bitcast.66), channel_id=1, replica_groups=mesh['row'=16,'col'=32] {'row'}, dimensions={0}, use_global_device_ids=true | all-gather | bytes 557056 | tf_op jit(solution)/shard_map/all_gather | solution.py:76
  88.2 3.4 %convolution_convert_fusion = bf16[256,2048]{0,1:T(8,128)(2,1)S(1)} fusion(bf16[2048,1024]{1,0:T(8,128)(2,1)} %bitcast.68, bf16[1024,256]{1,0:T(8,128)(2,1)S(1)} %all_gather.7), kind=kOutput, calls=%fused_computation | convolution fusion | flops 1074266112 | bytes 5767168 | tf_op jit(solution)/shard_map/dot_general | solution.py:77
  91.7 4.8 %fusion.39 = (bf16[1024,256]{1,0:T(8,128)(2,1)}, f32[1024,256]{1,0:T(8,128)S(1)}) fusion(bf16[2048,256]{1,0:T(8,128)(2,1)S(1)} %bitcast.64, bf16[2048,1024]{1,0:T(8,128)(2,1)} %bitcast.69), kind=kOutput, calls=%fused_computation.68 | convolution fusion | flops 1074003968 | bytes 6815744 | tf_op jit(solution)/shard_map/dot_general | solution.py:48
  96.4 0.8 fusion.41
  97.8 44.1 %all_to_all.20 = bf16[32,80,256]{2,1,0:T(8,128)(2,1)S(1)} all-to-all(bf16[32,80,256]{2,1,0:T(8,128)(2,1)S(1)} %pad_maximum_fusion), channel_id=1, replica_groups=mesh['row'=16,'col'=32] {'col'}, dimensions={0} | all-to-all | bytes 2621440 | tf_op jit(solution)/shard_map/all_to_all | solution.py:92
  141.9 6.1 %all-to-all-start.2 = ((bf16[16,64,256]{2,1,0:T(8,128)(2,1)}), bf16[16,64,256]{2,1,0:T(8,128)(2,1)S(1)}, u32[]{:S(2)}, u32[]{:S(2)}) async-start(bf16[16,64,256]{2,1,0:T(8,128)(2,1)} %bitcast.14), calls=%async_computation.2 | async-start | bytes 1048576 | tf_op jit(solution)/shard_map/all_to_all | solution.py:98
  148.1 25.7 %all-gather = f32[128,256]{1,0:T(8,128)S(1)} all-gather(f32[8,256]{1,0:T(8,128)S(1)} %add.24), channel_id=2, replica_groups=mesh['row'=16,'col'=32] {'row'}, dimensions={0}, use_global_device_ids=true | all-gather | bytes 139264 | tf_op jit(solution)/shard_map/all_gather | solution.py:103
  173.8 0.7 broadcast_in_dim.8
  174.6 3.9 %all-to-all-start.3 = ((f32[32,8,256]{2,1,0:T(8,128)}), f32[32,8,256]{2,1,0:T(8,128)S(1)}, u32[]{:S(2)}, u32[]{:S(2)}) async-start(f32[32,8,256]{2,1,0:T(8,128)} %broadcast_in_dim.8), calls=%async_computation.3 | async-start | bytes 524288 | tf_op jit(solution)/shard_map/all_to_all | solution.py:104
  178.7 0.9 fusion.27
  179.6 10.8 %all-to-all-done.3 = f32[32,8,256]{2,1,0:T(8,128)S(1)} async-done(((f32[32,8,256]{2,1,0:T(8,128)}), f32[32,8,256]{2,1,0:T(8,128)S(1)}, u32[]{:S(2)}, u32[]{:S(2)}) %all-to-all-start.3) | async-done | bytes 262176 | tf_op jit(solution)/shard_map/all_to_all | solution.py:104
  192.4 0.7 fusion.8
  (31 shorter events, 5.2 us)
Async XLA Ops:
  0.6 50.2 %copy-start = (f32[64,256]{1,0:T(8,128)S(1)}, f32[64,256]{1,0:T(8,128)}, u32[]{:S(2)}) copy-start(f32[64,256]{1,0:T(8,128)} %param.10) | copy-start | bytes 196612
  52.3 39.3 %all-to-all-start = ((bf16[32,64,256]{2,1,0:T(8,128)(2,1)}), bf16[32,64,256]{2,1,0:T(8,128)(2,1)S(1)}, u32[]{:S(2)}, u32[]{:S(2)}) async-start(bf16[32,64,256]{2,1,0:T(8,128)(2,1)} %broadcast_in_dim.7), calls=%async_computation | async-start | bytes 2097152 | tf_op jit(solution)/shard_map/all_to_all | solution.py:56
  91.7 5.7 %copy-start.2 = (f32[64,256]{1,0:T(8,128)S(1)}, f32[64,256]{1,0:T(8,128)}, u32[]{:S(2)}) copy-start(f32[64,256]{1,0:T(8,128)} %param.11) | copy-start | bytes 196612
  141.9 48.4 %copy-start.1 = (f32[256,256]{1,0:T(8,128)S(1)}, f32[256,256]{1,0:T(8,128)}, u32[]{:S(2)}) copy-start(f32[256,256]{1,0:T(8,128)} %param.9) | copy-start | bytes 786436
  141.9 31.9 %all-to-all-start.2 = ((bf16[16,64,256]{2,1,0:T(8,128)(2,1)}), bf16[16,64,256]{2,1,0:T(8,128)(2,1)S(1)}, u32[]{:S(2)}, u32[]{:S(2)}) async-start(bf16[16,64,256]{2,1,0:T(8,128)(2,1)} %bitcast.14), calls=%async_computation.2 | async-start | bytes 1048576 | tf_op jit(solution)/shard_map/all_to_all | solution.py:98
  174.6 15.8 %all-to-all-start.3 = ((f32[32,8,256]{2,1,0:T(8,128)}), f32[32,8,256]{2,1,0:T(8,128)S(1)}, u32[]{:S(2)}, u32[]{:S(2)}) async-start(f32[32,8,256]{2,1,0:T(8,128)} %broadcast_in_dim.8), calls=%async_computation.3 | async-start | bytes 524288 | tf_op jit(solution)/shard_map/all_to_all | solution.py:104

commit v12 on v11

--- a/solution.py
+++ b/solution.py
@@ -32,11 +32,11 @@
     highest = lax.Precision.HIGHEST
     half = square.shape[0] // 2
     first = lax.linalg.cholesky(square[:half, :half], symmetrize_input=False)
-    first_inv = invert_lower(first)
+    first_inv = with_layout_constraint(invert_lower(first), Layout((1, 0)))
     below = jnp.dot(square[half:, :half], first_inv.T, precision=highest)
     rest = square[half:, half:] - jnp.dot(below, below.T, precision=highest)
     last = lax.linalg.cholesky(rest, symmetrize_input=False)
-    last_inv = invert_lower(last)
+    last_inv = with_layout_constraint(invert_lower(last), Layout((1, 0)))
     corner = -jnp.dot(jnp.dot(last_inv, below, precision=highest), first_inv, precision=highest)
     zeros = jnp.zeros((half, square.shape[0] - half), square.dtype)
     factor = jnp.block([[first, zeros], [below, last]])

time: 194 us -> 193 us (level)
  transfers between devices with their start and end apart: 3 -> 3, of which waited for: 1 -> 1; matrix products, arithmetic and copies ran while one was open for 2% -> 3% of each run, Pallas kernels for 0% -> 0%
where the time goes in v12:
time: 193 us
  blocking collectives  95.2 us (49%)
  other arithmetic  47 us (24%)
  starting transfers between devices  20.4 us (11%)
  matrix products  15.6 us (8%)
  waiting for transfers between devices  10.7 us (6%)
  local copies, waits for them, and re-layouts  3.08 us (2%)
    all_to_all x1, blocking collectives, body(): got = lax.all_to_all(pieces, 'col', 0, 0, tiled=True)  44.1 us
    all_gather x1, blocking collectives, body(): lax.all_gather(coupling_col, 'row', axis=0, tiled=False).sum(0)  25.7 us
    all_gather x1, blocking collectives, body(): panel_cols = lax.all_gather(panel_own, 'row', axis=0, tiled=True)  25.4 us
    another operation x4, other arithmetic, invert_lower(): return lax.linalg.triangular_solve(factor, eye, left_side=True, lower=True)  21.1 us
    another operation x3, other arithmetic, factor_and_invert(): last = lax.linalg.cholesky(rest, symmetrize_input=False)  12.4 us
    another operation x3, other arithmetic, factor_and_invert(): first = lax.linalg.cholesky(square[:half, :half], symmetrize_input=False)  12.4 us
    all_to_all x1, waiting for transfers between devices, body(): lax.all_to_all(jnp.broadcast_to(coupling_rows[None], (n_col, strip, width...  10.7 us
    all_to_all x1, starting transfers between devices, gather_rows(): lax.all_to_all(spread, axis, 0, 0, tiled=True).reshape(-1, part.shape[-1])  10.5 us
  transfers between devices with their start and end apart: 3, of which 1 were waited for; matrix products, arithmetic and copies ran while one was open for 3% of the time, Pallas kernels for 0%

profile of v12, /device:TPU:1, one launch (start us, length us, event | category | flops | bytes accessed | tf_op | source)
XLA Modules:
  0.0 192.8 jit_solution(16815896537382374984)
XLA Ops:
  0.6 0.9 slice.22
  1.5 11.7 %custom-call.8 = f32[128,128]{1,0:T(8,128)S(1)} custom-call(f32[128,128]{1,0:T(8,128)S(1)} %slice.22), custom_call_target="Cholesky" | custom-call | tf_op jit(solution)/shard_map/cholesky/custom-call.1 | solution.py:34
  13.3 0.6 compare_reduce_fusion.1
  13.9 0.7 select_bitcast_fusion.1
  14.6 9.8 %custom-call.9 = f32[1,128,128]{1,2,0:T(8,128)S(1)} custom-call(f32[1,128,128]{2,1,0:T(8,128)S(1)} %get-tuple-element.8), custom_call_target="InvertDiagBlocksLowerTriangular" | custom-call | tf_op jit(solution)/shard_map/triangular_solve/custom-call.0 | solution.py:28
  24.7 1.1 fusion.30
  25.8 1.1 convolution_subtract_fusion.1
  26.9 11.7 %custom-call.10 = f32[128,128]{1,0:T(8,128)S(1)} custom-call(f32[128,128]{1,0:T(8,128)S(1)} %convolution_subtract_fusion.1), custom_call_target="Cholesky" | custom-call | tf_op jit(solution)/shard_map/cholesky/custom-call.1 | solution.py:38
  39.3 0.7 select_bitcast_fusion
  40.0 10.0 %custom-call.11 = f32[1,128,128]{1,2,0:T(8,128)S(1)} custom-call(f32[1,128,128]{2,1,0:T(8,128)S(1)} %get-tuple-element.6), custom_call_target="InvertDiagBlocksLowerTriangular" | custom-call | tf_op jit(solution)/shard_map/triangular_solve/custom-call.0 | solution.py:28
  51.1 1.1 broadcast_in_dim.7
  52.2 10.5 %all-to-all-start = ((bf16[32,64,256]{2,1,0:T(8,128)(2,1)}), bf16[32,64,256]{2,1,0:T(8,128)(2,1)S(1)}, u32[]{:S(2)}, u32[]{:S(2)}) async-start(bf16[32,64,256]{2,1,0:T(8,128)(2,1)} %broadcast_in_dim.7), calls=%async_computation | async-start | bytes 2097152 | tf_op jit(solution)/shard_map/all_to_all | solution.py:56
  62.7 25.4 %all_gather.7 = bf16[1024,256]{1,0:T(8,128)(2,1)S(1)} all-gather(bf16[64,256]{1,0:T(8,128)(2,1)S(1)} %bitcast.66), channel_id=1, replica_groups=mesh['row'=16,'col'=32] {'row'}, dimensions={0}, use_global_device_ids=true | all-gather | bytes 557056 | tf_op jit(solution)/shard_map/all_gather | solution.py:76
  88.1 3.4 %convolution_convert_fusion = bf16[256,2048]{0,1:T(8,128)(2,1)S(1)} fusion(bf16[2048,1024]{1,0:T(8,128)(2,1)} %bitcast.68, bf16[1024,256]{1,0:T(8,128)(2,1)S(1)} %all_gather.7), kind=kOutput, calls=%fused_computation | convolution fusion | flops 1074266112 | bytes 5767168 | tf_op jit(solution)/shard_map/dot_general | solution.py:77
  91.5 4.8 %fusion.39 = (bf16[1024,256]{1,0:T(8,128)(2,1)}, f32[1024,256]{1,0:T(8,128)S(1)}) fusion(bf16[2048,256]{1,0:T(8,128)(2,1)S(1)} %bitcast.64, bf16[2048,1024]{1,0:T(8,128)(2,1)} %bitcast.69), kind=kOutput, calls=%fused_computation.69 | convolution fusion | flops 1074003968 | bytes 6815744 | tf_op jit(solution)/shard_map/dot_general | solution.py:48
  96.3 0.8 fusion.41
  97.7 44.1 %all_to_all.20 = bf16[32,80,256]{2,1,0:T(8,128)(2,1)S(1)} all-to-all(bf16[32,80,256]{2,1,0:T(8,128)(2,1)S(1)} %pad_maximum_fusion), channel_id=1, replica_groups=mesh['row'=16,'col'=32] {'col'}, dimensions={0} | all-to-all | bytes 2621440 | tf_op jit(solution)/shard_map/all_to_all | solution.py:92
  141.8 6.1 %all-to-all-start.2 = ((bf16[16,64,256]{2,1,0:T(8,128)(2,1)}), bf16[16,64,256]{2,1,0:T(8,128)(2,1)S(1)}, u32[]{:S(2)}, u32[]{:S(2)}) async-start(bf16[16,64,256]{2,1,0:T(8,128)(2,1)} %bitcast.14), calls=%async_computation.2 | async-start | bytes 1048576 | tf_op jit(solution)/shard_map/all_to_all | solution.py:98
  148.0 25.7 %all-gather = f32[128,256]{1,0:T(8,128)S(1)} all-gather(f32[8,256]{1,0:T(8,128)S(1)} %add.24), channel_id=2, replica_groups=mesh['row'=16,'col'=32] {'row'}, dimensions={0}, use_global_device_ids=true | all-gather | bytes 139264 | tf_op jit(solution)/shard_map/all_gather | solution.py:103
  173.7 0.7 broadcast_in_dim.8
  174.4 3.9 %all-to-all-start.3 = ((f32[32,8,256]{2,1,0:T(8,128)}), f32[32,8,256]{2,1,0:T(8,128)S(1)}, u32[]{:S(2)}, u32[]{:S(2)}) async-start(f32[32,8,256]{2,1,0:T(8,128)} %broadcast_in_dim.8), calls=%async_computation.3 | async-start | bytes 524288 | tf_op jit(solution)/shard_map/all_to_all | solution.py:104
  178.6 1.0 fusion.27
  179.6 10.7 %all-to-all-done.3 = f32[32,8,256]{2,1,0:T(8,128)S(1)} async-done(((f32[32,8,256]{2,1,0:T(8,128)}), f32[32,8,256]{2,1,0:T(8,128)S(1)}, u32[]{:S(2)}, u32[]{:S(2)}) %all-to-all-start.3) | async-done | bytes 262176 | tf_op jit(solution)/shard_map/all_to_all | solution.py:104
  192.1 0.7 fusion.8
  (30 shorter events, 4.8 us)
Async XLA Ops:
  0.6 50.1 %copy-start = (f32[64,256]{1,0:T(8,128)S(1)}, f32[64,256]{1,0:T(8,128)}, u32[]{:S(2)}) copy-start(f32[64,256]{1,0:T(8,128)} %param.10) | copy-start | bytes 196612
  52.2 39.3 %all-to-all-start = ((bf16[32,64,256]{2,1,0:T(8,128)(2,1)}), bf16[32,64,256]{2,1,0:T(8,128)(2,1)S(1)}, u32[]{:S(2)}, u32[]{:S(2)}) async-start(bf16[32,64,256]{2,1,0:T(8,128)(2,1)} %broadcast_in_dim.7), calls=%async_computation | async-start | bytes 2097152 | tf_op jit(solution)/shard_map/all_to_all | solution.py:56
  91.5 5.7 %copy-start.2 = (f32[64,256]{1,0:T(8,128)S(1)}, f32[64,256]{1,0:T(8,128)}, u32[]{:S(2)}) copy-start(f32[64,256]{1,0:T(8,128)} %param.11) | copy-start | bytes 196612
  141.8 48.4 %copy-start.1 = (f32[256,256]{1,0:T(8,128)S(1)}, f32[256,256]{1,0:T(8,128)}, u32[]{:S(2)}) copy-start(f32[256,256]{1,0:T(8,128)} %param.9) | copy-start | bytes 786436
  141.8 31.9 %all-to-all-start.2 = ((bf16[16,64,256]{2,1,0:T(8,128)(2,1)}), bf16[16,64,256]{2,1,0:T(8,128)(2,1)S(1)}, u32[]{:S(2)}, u32[]{:S(2)}) async-start(bf16[16,64,256]{2,1,0:T(8,128)(2,1)} %bitcast.14), calls=%async_computation.2 | async-start | bytes 1048576 | tf_op jit(solution)/shard_map/all_to_all | solution.py:98
  174.4 15.8 %all-to-all-start.3 = ((f32[32,8,256]{2,1,0:T(8,128)}), f32[32,8,256]{2,1,0:T(8,128)S(1)}, u32[]{:S(2)}, u32[]{:S(2)}) async-start(f32[32,8,256]{2,1,0:T(8,128)} %broadcast_in_dim.8), calls=%async_computation.3 | async-start | bytes 524288 | tf_op jit(solution)/shard_map/all_to_all | solution.py:104
